TPU v7x, 256 devices: a whole 4x4x8 slice. The times are simulated.
256 devices in a mesh: sn: 64 (over y, z, core), rhs: 4 (over x).
Axes of the slice: x: 4, y: 4, z: 8, core: 2. Of those that a mesh axis runs over, the one named last changes fastest.
Arguments:
- leaf_rhs: float32 [256, 1024, 256], P('rhs', 'sn'), may hold values from -6 to 6
- root_rhs: float32 [256, 4096], P('rhs', 'sn'), may hold values from -6 to 6
- leaf_inverse: float32 [1024, 256, 256], P('sn'), as said below
- leaf_offdiagonal_block: float32 [1024, 128, 256], P('sn'), may hold values from -0.125 to 0.125
- update_rows: int32 [1024, 128], P('sn'), may hold values from 0 to 4095, as said below
- leaf_sizes: int32 [1024], P('sn'), may hold values from 1 to 256, 163840 in all
- root_inverse: float32 [4096, 4096], P('sn', 'rhs'), as said below
Outputs:
- leaf_solution: float32 [256, 1024, 256], P('rhs', 'sn')
- root_solution: float32 [256, 4096], P('rhs', 'sn')
Inputs may be any that keep to these rules, and one draw needn't show every extreme that they name: `update_rows`: the 128 rows of one leaf are distinct. `leaf_inverse`: lower triangular with a positive diagonal. `root_inverse`: lower triangular with a positive diagonal.
All inputs are finite; a program needn't handle non-finite values. No bound on the sum of `leaf_sizes` on one device may be relied on, other than what follows from the above.
Results may differ from a plain program's by a relative error of at most 0.00015.
Values sent between devices are 32-bit elements; how exact they have to be, the bound alone decides.
No kernel may reach another device: no remote copies, remote signals or barrier semaphores. Data moves between devices by JAX's collectives and lax.ppermute only.
A program may use at most 64 MiB of HBM per device.

v0:
```python
import jax
import jax.numpy as jnp
from jax import lax
from jax.sharding import Mesh
from jax.sharding import PartitionSpec as P

LEAF_AXES = ("y", "z", "core")


def owner_sum(parts):
    core = lax.axis_index("core")
    blocks = parts.shape[0]
    pairs = parts.reshape(blocks // 2, 2, *parts.shape[1:])
    mine = jnp.where(core == 1, pairs[:, 1], pairs[:, 0])
    other = jnp.where(core == 1, pairs[:, 0], pairs[:, 1])
    paired = mine + lax.ppermute(other, "core", [(0, 1), (1, 0)])
    spread = lax.all_to_all(paired, ("y", "z"), 0, 0, tiled=False)
    return spread.sum(0)


def share_all(block, blocks):
    width, columns = block.shape
    copies = jnp.broadcast_to(block[None], (blocks, width, columns))
    gathered = lax.all_to_all(copies, LEAF_AXES, 0, 0, tiled=False)
    return gathered.reshape(blocks * width, columns)


def on_device(
    leaf_rhs, root_rhs, leaf_inverse, leaf_offdiagonal_block, update_rows, leaf_sizes, root_inverse
):
    largest_entry = lax.Precision.HIGH
    leaf_count = leaf_inverse.shape[0]
    leaf_width = leaf_inverse.shape[1]
    touched = leaf_offdiagonal_block.shape[1]
    columns = leaf_rhs.shape[0]
    slot_index = lax.broadcasted_iota(jnp.int32, (leaf_count, leaf_width), 1)
    live_mask = (slot_index < leaf_sizes[:, None]).astype(jnp.float32)
    masked = leaf_inverse * live_mask[:, :, None] * live_mask[:, None, :]
    leaf_forward_sweep = jnp.einsum("clt,lst->cls", leaf_rhs, masked, precision=largest_entry)
    update_terms = jnp.einsum(
        "dwu,wqu->wqd", leaf_forward_sweep, leaf_offdiagonal_block, precision=largest_entry
    )
    root_full = lax.all_gather(root_inverse, "rhs", axis=1, tiled=True)
    root_order = root_full.shape[1]
    width = root_rhs.shape[1]
    blocks = root_order // width
    flat_rows = update_rows.reshape(-1)
    accumulated_sum = (
        jnp.zeros((root_order, columns), jnp.float32)
        .at[flat_rows]
        .add(update_terms.reshape(leaf_count * touched, columns))
    )
    shares = owner_sum(accumulated_sum.reshape(blocks, width, columns))
    reduced = root_rhs.T - shares
    forward_root = jnp.einsum(
        "jc,ij->ic",
        share_all(reduced, blocks),
        root_full,
        precision=largest_entry,
    )
    back_terms = jnp.einsum("ic,ij->jc", forward_root, root_full, precision=largest_entry)
    root_solution = owner_sum(back_terms.reshape(blocks, width, columns))
    root_values = share_all(root_solution, blocks)
    selected_rows = jnp.take(root_values, flat_rows, axis=0).reshape(leaf_count, touched, columns)
    adjusted_values = leaf_forward_sweep - jnp.einsum(
        "nvr,nvb->rnb", selected_rows, leaf_offdiagonal_block, precision=largest_entry
    )
    leaf_solution = jnp.einsum("cls,lst->clt", adjusted_values, masked, precision=largest_entry)
    return (leaf_solution, root_solution.T)


def solution(mesh):
    sn_size = mesh.shape["sn"]
    fine = Mesh(
        mesh.devices.reshape(sn_size // 16, 8, 2, mesh.shape["rhs"]), ("y", "z", "core", "rhs")
    )
    sn = LEAF_AXES
    in_specs = (
        P("rhs", sn, None),
        P("rhs", sn),
        P(sn, None, None),
        P(sn, None, None),
        P(sn, None),
        P(sn),
        P(sn, "rhs"),
    )
    out_specs = (P("rhs", sn, None), P("rhs", sn))
    return jax.shard_map(
        on_device, mesh=fine, in_specs=in_specs, out_specs=out_specs, check_vma=False
    )
```

profile of v0, /device:TPU:1, one launch (start us, length us, event | category | flops | bytes accessed | tf_op | source)
XLA Modules:
  0.0 241.4 jit_solution(5318736051149618329)
XLA Ops:
  8.1 5.3 %fusion.6 = f32[64,16,256]{2,0,1:T(8,128)S(1)} fusion(f32[16,256,256]{2,1,0:T(8,128)} %param.9, f32[16,256]{1,0:T(8,128)S(1)} %fusion.15, f32[64,16,256]{2,1,0:T(8,128)} %param.7), kind=kOutput, calls=%fused_computation.12 | convolution fusion | flops 404750336 | bytes 6307840 | tf_op jit(solution)/shard_map/clt,lst->cls/dot_general | solution.py:39
  16.9 13.3 %scatter_custom_fusion = f32[4096,64]{1,0:T(8,128)} fusion(s32[2048]{0:T(1024)S(1)} %bitcast.73, f32[2048,64]{1,0:T(8,128)} %bitcast.69, f32[]{:T(128)} %constant.27.clone.1), kind=kCustom, calls=%fused_computation.20 | custom fusion | flops 131072 | bytes 1049088 | tf_op jit(solution)/shard_map/scatter-add | solution.py:51
  30.2 3.1 %fusion.18 = (f32[32,1,64,64]{3,2,1,0:T(8,128)}, f32[32,1,64,64]{3,2,1,0:T(8,128)}) fusion(f32[32,2,64,64]{3,2,1,0:T(8,128)} %bitcast.65), kind=kLoop, calls=%fused_computation.34 | loop fusion | bytes 2097152 | tf_op jit(solution)/shard_map/slice | solution.py:14
  33.3 2.4 %copy.63 = f32[32,1,64,64]{2,1,0,3:T(1,128)S(1)} copy(f32[32,1,64,64]{3,2,1,0:T(8,128)} %get-tuple-element.13) | data formatting | bytes 1048576
  35.7 3.0 %copy.62 = f32[32,1,64,64]{2,0,3,1:T(8,128)} copy(f32[32,1,64,64]{3,2,1,0:T(8,128)} %get-tuple-element.12) | data formatting | bytes 1048576
  39.0 4.6 %collective-permute-start = (f32[32,64,64]{1,0,2:T(8,128)S(1)}, f32[32,64,64]{1,0,2:T(8,128)S(1)}, u32[]{:S(2)}, u32[]{:S(2)}) collective-permute-start(f32[32,64,64]{1,0,2:T(8,128)S(1)} %bitcast.70), channel_id=1, source_target_pairs={{0,4},{4,0},{1,5},{5,1},{2,6},{6,2},{3,7},{7,3},{8,12},{12,8},{9,1... | collective-permute-start | bytes 1572872 | tf_op jit(solution)/shard_map/ppermute | solution.py:16
  43.5 2.3 collective-permute-done
  48.3 23.7 %all_to_all.20 = f32[32,1,4096]{2,1,0:T(1,128)S(1)} all-to-all(f32[32,1,4096]{2,1,0:T(1,128)} %reshape.122), channel_id=1, replica_groups=mesh['y'=4,'z'=8,'core'=2,'rhs'=4] {'y','z'}, dimensions={0} | all-to-all | bytes 1048576 | tf_op jit(solution)/shard_map/all_to_all | solution.py:17
  72.5 2.7 %reduce = f32[32,4096]{1,0:T(8,128)} reduce(f32[32,1,4096]{2,1,0:T(1,128)S(1)} %all_to_all.20, f32[]{:T(128)} %broadcast.61), dimensions={1}, to_apply=%all_to_all.12.reduce_sub_computation | reduce | bytes 1048580 | tf_op jit(solution)/shard_map/all_to_all | solution.py:17
  76.8 1.6 broadcast_in_dim.15
  78.5 3.5 %reshape.124 = f32[64,1,4096]{2,1,0:T(1,128)} reshape(f32[64,64,64]{2,1,0:T(8,128)} %broadcast_in_dim.15) | data formatting | bytes 2097152
  81.9 9.6 %all-to-all-start.1 = ((f32[64,1,4096]{2,1,0:T(1,128)}), f32[64,1,4096]{2,1,0:T(1,128)}, u32[]{:S(2)}, u32[]{:S(2)}) async-start(f32[64,1,4096]{2,1,0:T(1,128)} %reshape.124), calls=%async_computation.1 | async-start | bytes 2097152 | tf_op jit(solution)/shard_map/all_to_all | solution.py:24
  92.3 27.7 %all-to-all-done.1 = f32[64,1,4096]{2,1,0:T(1,128)} async-done(((f32[64,1,4096]{2,1,0:T(1,128)}), f32[64,1,4096]{2,1,0:T(1,128)}, u32[]{:S(2)}, u32[]{:S(2)}) %all-to-all-start.1) | async-done | bytes 1048608 | tf_op jit(solution)/shard_map/all_to_all | solution.py:24
  120.0 4.3 %reduce.1 = f32[64,4096]{1,0:T(8,128)S(1)} reduce(f32[64,1,4096]{2,1,0:T(1,128)} %all-to-all-done.1, f32[]{:T(128)} %broadcast.61), dimensions={1}, to_apply=%all_to_all.13.reduce_sub_computation | reduce | bytes 2097156 | tf_op jit(solution)/shard_map/all_to_all | solution.py:24
  124.3 2.2 reshape.125
  126.5 3.7 %fusion.19 = f32[64,64]{1,0:T(8,128)S(1)} fusion(f32[4096,64]{1,0:T(8,128)} %bitcast.64, f32[64,4096]{1,0:T(8,128)} %all-gather.2.cloned.1.call-done), kind=kOutput, calls=%fused_computation.39 | convolution fusion | flops 100663296 | bytes 2113536 | tf_op jit(solution)/shard_map/jc,ij->ic/dot_general | solution.py:55
  130.8 2.9 %reshape_reshape.7 = f32[32,2,64,64]{2,1,0,3:T(2,128)} reshape(f32[4096,64]{0,1:T(8,128)S(1)} %convolution_bitcast_fusion) | data formatting | bytes 2097152 | tf_op jit(solution)/shard_map/reshape;reshape | solution.py:13
  133.7 4.4 %fusion.17 = (f32[32,1,64,64]{2,1,0,3:T(1,128)S(1)}, f32[32,1,64,64]{2,1,0,3:T(1,128)S(1)}) fusion(f32[32,2,64,64]{2,1,0,3:T(2,128)} %reshape_reshape.7), kind=kLoop, calls=%fused_computation.33 | loop fusion | bytes 2097152 | tf_op jit(solution)/shard_map/slice | solution.py:14
  138.5 2.6 %collective-permute-done.1 = f32[32,64,64]{1,0,2:T(8,128)S(1)} collective-permute-done((f32[32,64,64]{1,0,2:T(8,128)S(1)}, f32[32,64,64]{1,0,2:T(8,128)S(1)}, u32[]{:S(2)}, u32[]{:S(2)}) %collective-permute-start.1) | collective-permute-done | bytes 524320 | tf_op jit(solution)/shard_map/ppermute | solution.py:16
  143.5 19.6 %all_to_all.21 = f32[32,1,4096]{2,1,0:T(1,128)S(1)} all-to-all(f32[32,1,4096]{2,1,0:T(1,128)} %reshape.126), channel_id=1, replica_groups=mesh['y'=4,'z'=8,'core'=2,'rhs'=4] {'y','z'}, dimensions={0} | all-to-all | bytes 1048576 | tf_op jit(solution)/shard_map/all_to_all | solution.py:17
  163.1 2.7 %reduce.2 = f32[32,4096]{1,0:T(8,128)} reduce(f32[32,1,4096]{2,1,0:T(1,128)S(1)} %all_to_all.21, f32[]{:T(128)} %broadcast.61), dimensions={1}, to_apply=%all_to_all.14.reduce_sub_computation | reduce | bytes 1048580 | tf_op jit(solution)/shard_map/all_to_all | solution.py:17
  167.4 1.6 broadcast_in_dim.32
  169.1 3.4 %reshape.128 = f32[64,1,4096]{2,1,0:T(1,128)} reshape(f32[64,64,64]{2,1,0:T(8,128)} %broadcast_in_dim.32) | data formatting | bytes 2097152
  172.5 9.6 %all-to-all-start.3 = ((f32[64,1,4096]{2,1,0:T(1,128)}), f32[64,1,4096]{2,1,0:T(1,128)}, u32[]{:S(2)}, u32[]{:S(2)}) async-start(f32[64,1,4096]{2,1,0:T(1,128)} %reshape.128), calls=%async_computation.3 | async-start | bytes 2097152 | tf_op jit(solution)/shard_map/all_to_all | solution.py:24
  182.1 28.4 %all-to-all-done.3 = f32[64,1,4096]{2,1,0:T(1,128)} async-done(((f32[64,1,4096]{2,1,0:T(1,128)}), f32[64,1,4096]{2,1,0:T(1,128)}, u32[]{:S(2)}, u32[]{:S(2)}) %all-to-all-start.3) | async-done | bytes 1048608 | tf_op jit(solution)/shard_map/all_to_all | solution.py:24
  210.6 4.3 %reduce.3 = f32[64,4096]{1,0:T(8,128)S(1)} reduce(f32[64,1,4096]{2,1,0:T(1,128)} %all-to-all-done.3, f32[]{:T(128)} %broadcast.61), dimensions={1}, to_apply=%all_to_all.15.reduce_sub_computation | reduce | bytes 2097156 | tf_op jit(solution)/shard_map/all_to_all | solution.py:24
  214.9 2.2 reshape.129
  217.1 9.1 %gather_fusion = f32[2048,64]{1,0:T(8,128)} fusion(f32[4096,64]{1,0:T(8,128)} %bitcast.56, s32[2048]{0:T(1024)S(1)} %broadcast_clamp_fusion), kind=kCustom, calls=%fused_computation | custom fusion | bytes 1056768 | tf_op jit(solution)/shard_map/jit(_take)/gather | solution.py:64
  226.2 2.4 %copy.56 = f32[16,128,64]{1,2,0:T(8,128)} copy(f32[16,128,64]{2,1,0:T(8,128)} %bitcast.68) | data formatting | bytes 1048576 | tf_op jit(solution)/shard_map/jit(_take)/gather | solution.py:64
  228.7 1.9 fusion.8
  231.0 1.9 fusion.7
  232.9 1.6 copy.57
  (45 shorter events, 15.3 us)
Async XLA Ops:
  7.2 7.2 %copy-start = (f32[16,128,256]{2,1,0:T(8,128)S(1)}, f32[16,128,256]{2,1,0:T(8,128)}, u32[]{:S(2)}) copy-start(f32[16,128,256]{2,1,0:T(8,128)} %param.10) | copy-start | bytes 6291460
  13.4 1.0 copy-start.3
  14.4 2.5 %copy-start.8 = (s32[16,128]{1,0:T(8,128)S(1)}, s32[16,128]{1,0:T(8,128)}, u32[]{:S(2)}) copy-start(s32[16,128]{1,0:T(8,128)} %param.11) | copy-start | bytes 24580
  38.7 7.1 %copy-start.2 = (f32[32,1,64,64]{2,0,3,1:T(8,128)S(1)}, f32[32,1,64,64]{2,0,3,1:T(8,128)}, u32[]{:S(2)}) copy-start(f32[32,1,64,64]{2,0,3,1:T(8,128)} %copy.62) | copy-start | bytes 1572868
  39.0 6.9 %collective-permute-start = (f32[32,64,64]{1,0,2:T(8,128)S(1)}, f32[32,64,64]{1,0,2:T(8,128)S(1)}, u32[]{:S(2)}, u32[]{:S(2)}) collective-permute-start(f32[32,64,64]{1,0,2:T(8,128)S(1)} %bitcast.70), channel_id=1, source_target_pairs={{0,4},{4,0},{1,5},{5,1},{2,6},{6,2},{3,7},{7,3},{8,12},{12,8},{9,1... | collective-permute-start | bytes 1572872 | tf_op jit(solution)/shard_map/ppermute | solution.py:16
  71.9 4.8 %copy-start.7 = (f32[64,64]{1,0:T(8,128)S(1)}, f32[64,64]{1,0:T(8,128)}, u32[]{:S(2)}) copy-start(f32[64,64]{1,0:T(8,128)} %param.8) | copy-start | bytes 49156
  81.9 38.1 %all-to-all-start.1 = ((f32[64,1,4096]{2,1,0:T(1,128)}), f32[64,1,4096]{2,1,0:T(1,128)}, u32[]{:S(2)}, u32[]{:S(2)}) async-start(f32[64,1,4096]{2,1,0:T(1,128)} %reshape.124), calls=%async_computation.1 | async-start | bytes 2097152 | tf_op jit(solution)/shard_map/all_to_all | solution.py:24
  91.5 35.0 %all-gather.2.cloned.1.call-start = ((), (), s32[]{:S(2)}) async-start(), calls=%async_computation.4 | async-start | bytes 1310720 | tf_op jit(solution)/shard_map/all_gather | solution.py:43
  126.5 3.8 %copy-start.5 = (f32[64,4096]{1,0:T(8,128)S(1)}, f32[64,4096]{1,0:T(8,128)}, u32[]{:S(2)}) copy-start(f32[64,4096]{1,0:T(8,128)} %all-gather.2.cloned.1.call-done) | copy-start | bytes 3145732
  138.4 2.7 %collective-permute-start.1 = (f32[32,64,64]{1,0,2:T(8,128)S(1)}, f32[32,64,64]{1,0,2:T(8,128)S(1)}, u32[]{:S(2)}, u32[]{:S(2)}) collective-permute-start(f32[32,64,64]{1,0,2:T(8,128)S(1)} %select_bitcast_fusion), channel_id=1, source_target_pairs={{0,4},{4,0},{1,5},{5,1},{2,6},{6,2},{3,7},{7,3},{8,12},{12,8},{9,1... | collective-permute-start | bytes 1572872 | tf_op jit(solution)/shard_map/ppermute | solution.py:16
  167.4 5.2 %copy-start.6 = (f32[64,64]{0,1:T(8,128)}, f32[64,64]{0,1:T(8,128)S(1)}, u32[]{:S(2)}) copy-start(f32[64,64]{0,1:T(8,128)S(1)} %bitcast_reduce_fusion) | copy-start | bytes 49156
  172.5 38.1 %all-to-all-start.3 = ((f32[64,1,4096]{2,1,0:T(1,128)}), f32[64,1,4096]{2,1,0:T(1,128)}, u32[]{:S(2)}, u32[]{:S(2)}) async-start(f32[64,1,4096]{2,1,0:T(1,128)} %reshape.128), calls=%async_computation.3 | async-start | bytes 2097152 | tf_op jit(solution)/shard_map/all_to_all | solution.py:24
  226.2 2.4 %copy-start.4 = (f32[64,16,256]{2,0,1:T(8,128)S(1)}, f32[64,16,256]{2,0,1:T(8,128)}, u32[]{:S(2)}) copy-start(f32[64,16,256]{2,0,1:T(8,128)} %copy-done.3) | copy-start | bytes 3145732
  228.7 2.3 copy-start.1
Sparse Core Ops, SparseCore 0:
  94.2 25.6 all-gather.1
where the time goes:
time: 242 us; the launch traced here: 241 us
  waiting for transfers between devices  61.7 us (25%)
  local copies, waits for them, and re-layouts  53.9 us (22%)
  blocking collectives  43.2 us (18%)
  other arithmetic  29.6 us (12%)
  starting transfers between devices  24 us (10%)
  matrix products  14.7 us (6%)
  between operations  14.2 us (6%)
    all_to_all x2, waiting for transfers between devices, share_all(): gathered = lax.all_to_all(copies, LEAF_AXES, 0, 0, tiled=False)  56.1 us
    all_to_all x2, blocking collectives, owner_sum(): spread = lax.all_to_all(paired, ('y', 'z'), 0, 0, tiled=False)  43.2 us
    unnamed x29, local copies, waits for them, and re-layouts  25.5 us
    all_to_all x2, starting transfers between devices, share_all(): gathered = lax.all_to_all(copies, LEAF_AXES, 0, 0, tiled=False)  19.2 us
    scatter-add x1, other arithmetic, on_device(): accumulated_sum = jnp.zeros((root_order, columns), jnp.float32).at[flat_r...  13.3 us
    gather x2, local copies, waits for them, and re-layouts, on_device(): jnp.take(root_values, flat_rows, axis=0)  11.6 us
    all_to_all x2, other arithmetic, share_all(): gathered = lax.all_to_all(copies, LEAF_AXES, 0, 0, tiled=False)  8.7 us
    slice x2, local copies, waits for them, and re-layouts, owner_sum(): mine = jnp.where(core == 1, pairs[:, 1], pairs[:, 0])  7.51 us
  transfers between devices with their start and end apart: 5, of which 4 were waited for; matrix products, arithmetic and copies ran while one was open for 3% of the time, Pallas kernels for 0%

commit v1 on v0

--- a/solution.py
+++ b/solution.py
@@ -9,18 +9,19 @@
 
 def owner_sum(parts):
     core = lax.axis_index("core")
-    blocks = parts.shape[0]
-    pairs = parts.reshape(blocks // 2, 2, *parts.shape[1:])
+    blocks, width, columns = parts.shape
+    pairs = parts.reshape(blocks // 2, 2, 8, width * columns // 8)
     mine = jnp.where(core == 1, pairs[:, 1], pairs[:, 0])
     other = jnp.where(core == 1, pairs[:, 0], pairs[:, 1])
     paired = mine + lax.ppermute(other, "core", [(0, 1), (1, 0)])
     spread = lax.all_to_all(paired, ("y", "z"), 0, 0, tiled=False)
-    return spread.sum(0)
+    return spread.sum(0).reshape(width, columns)
 
 
 def share_all(block, blocks):
     width, columns = block.shape
-    copies = jnp.broadcast_to(block[None], (blocks, width, columns))
+    flat = block.reshape(1, 8, width * columns // 8)
+    copies = jnp.broadcast_to(flat, (blocks, 8, width * columns // 8))
     gathered = lax.all_to_all(copies, LEAF_AXES, 0, 0, tiled=False)
     return gathered.reshape(blocks * width, columns)
 

time: 242 us -> 203 us (0.84)
  local copies, waits for them, and re-layouts: 53.9 us -> 28.4 us
  blocking collectives: 43.2 us -> 23.6 us
  other arithmetic: 29.6 us -> 15.5 us
  waiting for transfers between devices: 61.7 us -> 73.4 us
  starting transfers between devices: 24 us -> 32.5 us
    unnamed x29 -> x17, local copies, waits for them, and re-layouts: 25.5 us -> 3.79 us
    all_to_all x2 -> x1, blocking collectives: 43.2 us -> 23.6 us  [owner_sum(): spread = lax.all_to_all(paired, ('y', 'z'), 0, 0, tiled=False)]
    all_to_all x4 -> x0, other arithmetic: 14.1 us -> none  [the longest x2 8.7 us: share_all(): gathered = lax.all_to_all(copies, LEAF_AXES, 0, 0, tiled=False)]
    all_to_all x0 -> x1, waiting for transfers between devices: none -> 14.1 us  [owner_sum(): spread = lax.all_to_all(paired, ('y', 'z'), 0, 0, tiled=False)]
    all_to_all x0 -> x1, starting transfers between devices: none -> 9.5 us  [owner_sum(): spread = lax.all_to_all(paired, ('y', 'z'), 0, 0, tiled=False)]
    slice x2 -> x0, local copies, waits for them, and re-layouts: 7.51 us -> none  [owner_sum(): mine = jnp.where(core == 1, pairs[:, 1], pairs[:, 0])]
    reshape x0 -> x4, local copies, waits for them, and re-layouts: none -> 3.67 us  [the longest x2 3.52 us: share_all(): return gathered.reshape(blocks * width, columns)]
  transfers between devices with their start and end apart: 5 -> 6, of which waited for: 4 -> 5; matrix products, arithmetic and copies ran while one was open for 3% -> 1% of each run, Pallas kernels for 0% -> 0%
where the time goes in v1:
time: 203 us; the launch traced here: 202 us
  waiting for transfers between devices  73.4 us (36%)
  starting transfers between devices  32.5 us (16%)
  local copies, waits for them, and re-layouts  28.4 us (14%)
  blocking collectives  23.6 us (12%)
  other arithmetic  15.5 us (8%)
  matrix products  14.7 us (7%)
  between operations  14.2 us (7%)
    all_to_all x2, waiting for transfers between devices, share_all(): gathered = lax.all_to_all(copies, LEAF_AXES, 0, 0, tiled=False)  55.5 us
    all_to_all x1, blocking collectives, owner_sum(): spread = lax.all_to_all(paired, ('y', 'z'), 0, 0, tiled=False)  23.6 us
    all_to_all x2, starting transfers between devices, share_all(): gathered = lax.all_to_all(copies, LEAF_AXES, 0, 0, tiled=False)  18.8 us
    all_to_all x1, waiting for transfers between devices, owner_sum(): spread = lax.all_to_all(paired, ('y', 'z'), 0, 0, tiled=False)  14.1 us
    scatter-add x1, other arithmetic, on_device(): accumulated_sum = jnp.zeros((root_order, columns), jnp.float32).at[flat_r...  13.3 us
    gather x2, local copies, waits for them, and re-layouts, on_device(): jnp.take(root_values, flat_rows, axis=0)  11.6 us
    all_to_all x1, starting transfers between devices, owner_sum(): spread = lax.all_to_all(paired, ('y', 'z'), 0, 0, tiled=False)  9.5 us
    dot_general x1, matrix products, on_device(): jnp.einsum('clt,lst->cls', leaf_rhs, masked, precision=largest_entry)  5.35 us
  transfers between devices with their start and end apart: 6, of which 5 were waited for; matrix products, arithmetic and copies ran while one was open for 1% of the time, Pallas kernels for 0%

profile of v1, /device:TPU:1, one launch (start us, length us, event | category | flops | bytes accessed | tf_op | source)
XLA Modules:
  0.0 202.3 jit_solution(5000113157473604307)
XLA Ops:
  7.2 0.9 fusion.17
  8.1 5.3 %fusion.6 = f32[64,16,256]{2,0,1:T(8,128)S(1)} fusion(f32[16,256,256]{2,1,0:T(8,128)} %param.9, f32[16,256]{1,0:T(8,128)S(1)} %fusion.17, f32[64,16,256]{2,1,0:T(8,128)} %param.7), kind=kOutput, calls=%fused_computation.11 | convolution fusion | flops 404750336 | bytes 6307840 | tf_op jit(solution)/shard_map/clt,lst->cls/dot_general | solution.py:40
  13.4 1.0 copy-done.2
  14.4 1.2 convolution_bitcast_fusion.2
  15.6 1.3 copy.43
  16.9 13.3 %scatter_custom_fusion = f32[4096,64]{1,0:T(8,128)} fusion(s32[2048]{0:T(1024)S(1)} %bitcast.65, f32[2048,64]{1,0:T(8,128)} %bitcast.62, f32[]{:T(128)} %constant.27.clone.1), kind=kCustom, calls=%fused_computation.16 | custom fusion | flops 131072 | bytes 1049088 | tf_op jit(solution)/shard_map/scatter-add | solution.py:52
  30.2 1.9 reshape_reshape.7
  32.2 3.3 %collective-permute-start = (f32[32,8,512]{2,1,0:T(8,128)S(1)}, f32[32,8,512]{2,1,0:T(8,128)S(1)}, u32[]{:S(2)}, u32[]{:S(2)}) collective-permute-start(f32[32,8,512]{2,1,0:T(8,128)S(1)} %select_bitcast_fusion.1), channel_id=1, source_target_pairs={{0,4},{4,0},{1,5},{5,1},{2,6},{6,2},{3,7},{7,3},{8,12},{12,8},{9,1... | collective-permute-start | bytes 1572872 | tf_op jit(solution)/shard_map/ppermute | solution.py:16
  35.5 1.5 collective-permute-done
  37.1 0.9 fusion.13
  38.0 9.5 %all-to-all-start = ((f32[32,8,512]{2,1,0:T(8,128)}), f32[32,8,512]{2,1,0:T(8,128)S(1)}, u32[]{:S(2)}, u32[]{:S(2)}) async-start(f32[32,8,512]{2,1,0:T(8,128)} %fusion.13), calls=%async_computation | async-start | bytes 1048576 | tf_op jit(solution)/shard_map/all_to_all | solution.py:17
  47.6 14.1 %all-to-all-done = f32[32,8,512]{2,1,0:T(8,128)S(1)} async-done(((f32[32,8,512]{2,1,0:T(8,128)}), f32[32,8,512]{2,1,0:T(8,128)S(1)}, u32[]{:S(2)}, u32[]{:S(2)}) %all-to-all-start) | async-done | bytes 524320 | tf_op jit(solution)/shard_map/all_to_all | solution.py:17
  61.9 1.1 broadcast_in_dim.32
  63.0 9.4 %all-to-all-start.1 = ((f32[64,8,512]{2,1,0:T(8,128)}), f32[64,8,512]{2,1,0:T(8,128)S(1)}, u32[]{:S(2)}, u32[]{:S(2)}) async-start(f32[64,8,512]{2,1,0:T(8,128)} %broadcast_in_dim.32), calls=%async_computation.1 | async-start | bytes 2097152 | tf_op jit(solution)/shard_map/all_to_all | solution.py:25
  73.2 27.8 %all-to-all-done.1 = f32[64,8,512]{2,1,0:T(8,128)S(1)} async-done(((f32[64,8,512]{2,1,0:T(8,128)}), f32[64,8,512]{2,1,0:T(8,128)S(1)}, u32[]{:S(2)}, u32[]{:S(2)}) %all-to-all-start.1) | async-done | bytes 1048608 | tf_op jit(solution)/shard_map/all_to_all | solution.py:25
  100.9 1.8 reshape.110
  102.7 3.7 %fusion.19 = f32[64,64]{1,0:T(8,128)S(1)} fusion(f32[4096,64]{1,0:T(8,128)} %reshape.110, f32[64,4096]{1,0:T(8,128)} %all-gather.2.cloned.1.call-done), kind=kOutput, calls=%fused_computation.37 | convolution fusion | flops 100663296 | bytes 2113536 | tf_op jit(solution)/shard_map/jc,ij->ic/dot_general | solution.py:56
  107.0 1.9 copy.37
  109.0 1.9 reshape_reshape.8
  111.0 0.9 collective-permute-start.1
  111.9 1.5 collective-permute-done.1
  113.6 23.6 %all_to_all.20 = f32[32,8,512]{2,1,0:T(8,128)S(1)} all-to-all(f32[32,8,512]{2,1,0:T(8,128)S(1)} %bitcast_add_fusion), channel_id=1, replica_groups=mesh['y'=4,'z'=8,'core'=2,'rhs'=4] {'y','z'}, dimensions={0} | all-to-all | bytes 1048576 | tf_op jit(solution)/shard_map/all_to_all | solution.py:17
  137.2 1.1 broadcast_in_dim.33
  138.3 9.4 %all-to-all-start.3 = ((f32[64,8,512]{2,1,0:T(8,128)}), f32[64,8,512]{2,1,0:T(8,128)S(1)}, u32[]{:S(2)}, u32[]{:S(2)}) async-start(f32[64,8,512]{2,1,0:T(8,128)} %broadcast_in_dim.33), calls=%async_computation.3 | async-start | bytes 2097152 | tf_op jit(solution)/shard_map/all_to_all | solution.py:25
  147.8 0.7 copy.42
  148.5 27.7 %all-to-all-done.3 = f32[64,8,512]{2,1,0:T(8,128)S(1)} async-done(((f32[64,8,512]{2,1,0:T(8,128)}), f32[64,8,512]{2,1,0:T(8,128)S(1)}, u32[]{:S(2)}, u32[]{:S(2)}) %all-to-all-start.3) | async-done | bytes 1048608 | tf_op jit(solution)/shard_map/all_to_all | solution.py:25
  176.2 1.8 reshape.111
  178.0 9.1 %gather_fusion = f32[2048,64]{1,0:T(8,128)} fusion(f32[4096,64]{1,0:T(8,128)} %reshape.111, s32[2048]{0:T(1024)S(1)} %broadcast_clamp_fusion), kind=kCustom, calls=%fused_computation | custom fusion | bytes 1056768 | tf_op jit(solution)/shard_map/jit(_take)/gather | solution.py:65
  187.2 2.4 %copy.40 = f32[16,128,64]{1,2,0:T(8,128)} copy(f32[16,128,64]{2,1,0:T(8,128)} %bitcast.61) | data formatting | bytes 1048576 | tf_op jit(solution)/shard_map/jit(_take)/gather | solution.py:65
  189.6 1.9 fusion.8
  191.9 1.9 fusion.7
  193.8 1.6 copy.41
  (30 shorter events, 2.5 us)
Async XLA Ops:
  7.2 7.2 %copy-start = (f32[16,128,256]{2,1,0:T(8,128)S(1)}, f32[16,128,256]{2,1,0:T(8,128)}, u32[]{:S(2)}) copy-start(f32[16,128,256]{2,1,0:T(8,128)} %param.10) | copy-start | bytes 6291460
  13.4 1.0 copy-start.2
  14.4 2.5 %copy-start.5 = (s32[16,128]{1,0:T(8,128)S(1)}, s32[16,128]{1,0:T(8,128)}, u32[]{:S(2)}) copy-start(s32[16,128]{1,0:T(8,128)} %param.11) | copy-start | bytes 24580
  32.1 15.4 %copy-start.6 = (f32[64,64]{1,0:T(8,128)S(1)}, f32[64,64]{1,0:T(8,128)}, u32[]{:S(2)}) copy-start(f32[64,64]{1,0:T(8,128)} %param.8) | copy-start | bytes 49156
  32.2 4.8 %collective-permute-start = (f32[32,8,512]{2,1,0:T(8,128)S(1)}, f32[32,8,512]{2,1,0:T(8,128)S(1)}, u32[]{:S(2)}, u32[]{:S(2)}) collective-permute-start(f32[32,8,512]{2,1,0:T(8,128)S(1)} %select_bitcast_fusion.1), channel_id=1, source_target_pairs={{0,4},{4,0},{1,5},{5,1},{2,6},{6,2},{3,7},{7,3},{8,12},{12,8},{9,1... | collective-permute-start | bytes 1572872 | tf_op jit(solution)/shard_map/ppermute | solution.py:16
  38.0 23.7 %all-to-all-start = ((f32[32,8,512]{2,1,0:T(8,128)}), f32[32,8,512]{2,1,0:T(8,128)S(1)}, u32[]{:S(2)}, u32[]{:S(2)}) async-start(f32[32,8,512]{2,1,0:T(8,128)} %fusion.13), calls=%async_computation | async-start | bytes 1048576 | tf_op jit(solution)/shard_map/all_to_all | solution.py:17
  63.0 37.9 %all-to-all-start.1 = ((f32[64,8,512]{2,1,0:T(8,128)}), f32[64,8,512]{2,1,0:T(8,128)S(1)}, u32[]{:S(2)}, u32[]{:S(2)}) async-start(f32[64,8,512]{2,1,0:T(8,128)} %broadcast_in_dim.32), calls=%async_computation.1 | async-start | bytes 2097152 | tf_op jit(solution)/shard_map/all_to_all | solution.py:25
  72.4 30.3 %all-gather.2.cloned.1.call-start = ((), (), s32[]{:S(2)}) async-start(), calls=%async_computation.4 | async-start | bytes 1310720 | tf_op jit(solution)/shard_map/all_gather | solution.py:44
  102.7 3.8 %copy-start.4 = (f32[64,4096]{1,0:T(8,128)S(1)}, f32[64,4096]{1,0:T(8,128)}, u32[]{:S(2)}) copy-start(f32[64,4096]{1,0:T(8,128)} %all-gather.2.cloned.1.call-done) | copy-start | bytes 3145732
  111.0 2.4 %collective-permute-start.1 = (f32[32,8,512]{2,1,0:T(8,128)S(1)}, f32[32,8,512]{2,1,0:T(8,128)S(1)}, u32[]{:S(2)}, u32[]{:S(2)}) collective-permute-start(f32[32,8,512]{2,1,0:T(8,128)S(1)} %select_bitcast_fusion), channel_id=1, source_target_pairs={{0,4},{4,0},{1,5},{5,1},{2,6},{6,2},{3,7},{7,3},{8,12},{12,8},{9,1... | collective-permute-start | bytes 1572872 | tf_op jit(solution)/shard_map/ppermute | solution.py:16
  138.3 37.9 %all-to-all-start.3 = ((f32[64,8,512]{2,1,0:T(8,128)}), f32[64,8,512]{2,1,0:T(8,128)S(1)}, u32[]{:S(2)}, u32[]{:S(2)}) async-start(f32[64,8,512]{2,1,0:T(8,128)} %broadcast_in_dim.33), calls=%async_computation.3 | async-start | bytes 2097152 | tf_op jit(solution)/shard_map/all_to_all | solution.py:25
  187.2 2.4 %copy-start.3 = (f32[64,16,256]{2,0,1:T(8,128)S(1)}, f32[64,16,256]{2,0,1:T(8,128)}, u32[]{:S(2)}) copy-start(f32[64,16,256]{2,0,1:T(8,128)} %copy-done.2) | copy-start | bytes 3145732
  189.6 2.3 %copy-start.1 = (f32[16,256,256]{2,1,0:T(8,128)S(1)}, f32[16,256,256]{2,1,0:T(8,128)}, u32[]{:S(2)}) copy-start(f32[16,256,256]{2,1,0:T(8,128)} %param.9) | copy-start | bytes 12582916
Sparse Core Ops, SparseCore 0:
  75.0 25.6 all-gather.1

commit v2 on v1

--- a/solution.py
+++ b/solution.py
@@ -20,9 +20,12 @@
 
 def share_all(block, blocks):
     width, columns = block.shape
-    flat = block.reshape(1, 8, width * columns // 8)
-    copies = jnp.broadcast_to(flat, (blocks, 8, width * columns // 8))
-    gathered = lax.all_to_all(copies, LEAF_AXES, 0, 0, tiled=False)
+    core = lax.axis_index("core")
+    flat = block.reshape(8, width * columns // 8)
+    partner = lax.ppermute(flat, "core", [(0, 1), (1, 0)])
+    pair = jnp.where(core == 1, jnp.stack([partner, flat]), jnp.stack([flat, partner]))
+    copies = jnp.broadcast_to(pair[None], (blocks // 2, *pair.shape))
+    gathered = lax.all_to_all(copies, ("y", "z"), 0, 0, tiled=False)
     return gathered.reshape(blocks * width, columns)
 
 

time: 203 us -> 203 us (level); the launches traced: 202 us -> 200 us
  waiting for transfers between devices: 73.4 us -> 70 us
    all_to_all x2, starting transfers between devices: 18.8 us -> 10.9 us  [share_all(): gathered = lax.all_to_all(copies, ('y', 'z'), 0, 0, tiled=False)]
    ppermute x0 -> x2, starting transfers between devices: none -> 7.12 us  [share_all(): partner = lax.ppermute(flat, 'core', [(0, 1), (1, 0)])]
    all_to_all x2, waiting for transfers between devices: 55.5 us -> 48.9 us  [share_all(): gathered = lax.all_to_all(copies, ('y', 'z'), 0, 0, tiled=False)]
    ppermute x2, starting transfers between devices: 4.18 us -> 6.25 us  [owner_sum(): paired = mine + lax.ppermute(other, 'core', [(0, 1), (1, 0)])]
  transfers between devices with their start and end apart: 6 -> 8, of which waited for: 5 -> 8; matrix products, arithmetic and copies ran while one was open for 1% -> 1% of each run, Pallas kernels for 0% -> 0%
where the time goes in v2:
time: 203 us; the launch traced here: 200 us
  waiting for transfers between devices  70 us (34%)
  starting transfers between devices  33.8 us (17%)
  local copies, waits for them, and re-layouts  28.5 us (14%)
  blocking collectives  23.4 us (12%)
  other arithmetic  15.5 us (8%)
  matrix products  14.7 us (7%)
  between operations  14.2 us (7%)
    all_to_all x2, waiting for transfers between devices, share_all(): gathered = lax.all_to_all(copies, ('y', 'z'), 0, 0, tiled=False)  48.9 us
    all_to_all x1, blocking collectives, owner_sum(): spread = lax.all_to_all(paired, ('y', 'z'), 0, 0, tiled=False)  23.4 us
    all_to_all x1, waiting for transfers between devices, owner_sum(): spread = lax.all_to_all(paired, ('y', 'z'), 0, 0, tiled=False)  14.1 us
    scatter-add x1, other arithmetic, on_device(): accumulated_sum = jnp.zeros((root_order, columns), jnp.float32).at[flat_r...  13.2 us
    gather x2, local copies, waits for them, and re-layouts, on_device(): jnp.take(root_values, flat_rows, axis=0)  11.6 us
    all_to_all x2, starting transfers between devices, share_all(): gathered = lax.all_to_all(copies, ('y', 'z'), 0, 0, tiled=False)  10.9 us
    all_to_all x1, starting transfers between devices, owner_sum(): spread = lax.all_to_all(paired, ('y', 'z'), 0, 0, tiled=False)  9.5 us
    ppermute x2, starting transfers between devices, share_all(): partner = lax.ppermute(flat, 'core', [(0, 1), (1, 0)])  7.12 us
  transfers between devices with their start and end apart: 8, of which 8 were waited for; matrix products, arithmetic and copies ran while one was open for 1% of the time, Pallas kernels for 0%

profile of v2, /device:TPU:1, one launch (start us, length us, event | category | flops | bytes accessed | tf_op | source)
XLA Modules:
  0.0 200.1 jit_solution(51407674050059758)
XLA Ops:
  8.1 5.3 %fusion.6 = f32[64,16,256]{2,0,1:T(8,128)S(1)} fusion(f32[16,256,256]{2,1,0:T(8,128)} %param.9, f32[16,256]{1,0:T(8,128)S(1)} %fusion.17, f32[64,16,256]{2,1,0:T(8,128)} %param.7), kind=kOutput, calls=%fused_computation.11 | convolution fusion | flops 404750336 | bytes 6307840 | tf_op jit(solution)/shard_map/clt,lst->cls/dot_general | solution.py:43
  13.4 1.0 copy-done.2
  14.4 1.2 convolution_bitcast_fusion.2
  15.6 1.3 copy.43
  16.9 13.2 %scatter_custom_fusion = f32[4096,64]{1,0:T(8,128)} fusion(s32[2048]{0:T(1024)S(1)} %bitcast.73, f32[2048,64]{1,0:T(8,128)} %bitcast.69, f32[]{:T(128)} %constant.27.clone.1), kind=kCustom, calls=%fused_computation.16 | custom fusion | flops 131072 | bytes 1049088 | tf_op jit(solution)/shard_map/scatter-add | solution.py:55
  30.2 1.9 reshape_reshape.6
  32.2 3.3 %collective-permute-start = (f32[32,8,512]{2,1,0:T(8,128)S(1)}, f32[32,8,512]{2,1,0:T(8,128)S(1)}, u32[]{:S(2)}, u32[]{:S(2)}) collective-permute-start(f32[32,8,512]{2,1,0:T(8,128)S(1)} %select_bitcast_fusion.1), channel_id=1, source_target_pairs={{0,4},{4,0},{1,5},{5,1},{2,6},{6,2},{3,7},{7,3},{8,12},{12,8},{9,1... | collective-permute-start | bytes 1572872 | tf_op jit(solution)/shard_map/ppermute | solution.py:16
  35.5 1.5 collective-permute-done
  38.0 9.5 %all-to-all-start = ((f32[32,8,512]{2,1,0:T(8,128)}), f32[32,8,512]{2,1,0:T(8,128)S(1)}, u32[]{:S(2)}, u32[]{:S(2)}) async-start(f32[32,8,512]{2,1,0:T(8,128)} %fusion.13), calls=%async_computation | async-start | bytes 1048576 | tf_op jit(solution)/shard_map/all_to_all | solution.py:17
  47.6 14.1 %all-to-all-done = f32[32,8,512]{2,1,0:T(8,128)S(1)} async-done(((f32[32,8,512]{2,1,0:T(8,128)}), f32[32,8,512]{2,1,0:T(8,128)S(1)}, u32[]{:S(2)}, u32[]{:S(2)}) %all-to-all-start) | async-done | bytes 524320 | tf_op jit(solution)/shard_map/all_to_all | solution.py:17
  61.9 3.5 %collective-permute-start.1 = (f32[8,512]{1,0:T(8,128)S(1)}, f32[8,512]{1,0:T(8,128)S(1)}, u32[]{:S(2)}, u32[]{:S(2)}) collective-permute-start(f32[8,512]{1,0:T(8,128)S(1)} %reshape.176), channel_id=1, source_target_pairs={{0,4},{4,0},{1,5},{5,1},{2,6},{6,2},{3,7},{7,3},{8,12},{12,8},{9,1... | collective-permute-start | bytes 49160 | tf_op jit(solution)/shard_map/ppermute | solution.py:25
  66.3 1.1 broadcast_in_dim.15
  67.4 5.5 %all-to-all-start.1 = ((f32[32,2,8,512]{3,2,1,0:T(8,128)}), f32[32,2,8,512]{3,2,1,0:T(8,128)S(1)}, u32[]{:S(2)}, u32[]{:S(2)}) async-start(f32[32,2,8,512]{3,2,1,0:T(8,128)} %broadcast_in_dim.15), calls=%async_computation.1 | async-start | bytes 2097152 | tf_op jit(solution)/shard_map/all_to_all | solution.py:28
  73.6 24.5 %all-to-all-done.1 = f32[32,2,8,512]{3,2,1,0:T(8,128)S(1)} async-done(((f32[32,2,8,512]{3,2,1,0:T(8,128)}), f32[32,2,8,512]{3,2,1,0:T(8,128)S(1)}, u32[]{:S(2)}, u32[]{:S(2)}) %all-to-all-start.1) | async-done | bytes 1048608 | tf_op jit(solution)/shard_map/all_to_all | solution.py:28
  98.1 1.7 reshape.177
  99.8 1.6 all-gather.2.cloned.1.call-done
  101.5 3.7 %fusion.19 = f32[64,64]{1,0:T(8,128)S(1)} fusion(f32[4096,64]{1,0:T(8,128)} %reshape.177, f32[64,4096]{1,0:T(8,128)} %all-gather.2.cloned.1.call-done), kind=kOutput, calls=%fused_computation.39 | convolution fusion | flops 100663296 | bytes 2113536 | tf_op jit(solution)/shard_map/jc,ij->ic/dot_general | solution.py:59
  105.8 1.9 copy.37
  107.7 1.9 reshape_reshape.7
  109.7 3.0 %collective-permute-start.2 = (f32[32,8,512]{2,1,0:T(8,128)S(1)}, f32[32,8,512]{2,1,0:T(8,128)S(1)}, u32[]{:S(2)}, u32[]{:S(2)}) collective-permute-start(f32[32,8,512]{2,1,0:T(8,128)S(1)} %select_bitcast_fusion), channel_id=1, source_target_pairs={{0,4},{4,0},{1,5},{5,1},{2,6},{6,2},{3,7},{7,3},{8,12},{12,8},{9,1... | collective-permute-start | bytes 1572872 | tf_op jit(solution)/shard_map/ppermute | solution.py:16
  112.7 1.5 collective-permute-done.2
  114.4 23.4 %all_to_all.20 = f32[32,8,512]{2,1,0:T(8,128)S(1)} all-to-all(f32[32,8,512]{2,1,0:T(8,128)S(1)} %bitcast_add_fusion), channel_id=1, replica_groups=mesh['y'=4,'z'=8,'core'=2,'rhs'=4] {'y','z'}, dimensions={0} | all-to-all | bytes 1048576 | tf_op jit(solution)/shard_map/all_to_all | solution.py:17
  137.9 3.6 %collective-permute-start.3 = (f32[8,512]{1,0:T(8,128)S(1)}, f32[8,512]{1,0:T(8,128)S(1)}, u32[]{:S(2)}, u32[]{:S(2)}) collective-permute-start(f32[8,512]{1,0:T(8,128)S(1)} %reduce_sum.19), channel_id=1, source_target_pairs={{0,4},{4,0},{1,5},{5,1},{2,6},{6,2},{3,7},{7,3},{8,12},{12,8},{9,1... | collective-permute-start | bytes 49160 | tf_op jit(solution)/shard_map/ppermute | solution.py:25
  142.3 1.1 broadcast_in_dim.32
  143.4 5.5 %all-to-all-start.3 = ((f32[32,2,8,512]{3,2,1,0:T(8,128)}), f32[32,2,8,512]{3,2,1,0:T(8,128)S(1)}, u32[]{:S(2)}, u32[]{:S(2)}) async-start(f32[32,2,8,512]{3,2,1,0:T(8,128)} %broadcast_in_dim.32), calls=%async_computation.3 | async-start | bytes 2097152 | tf_op jit(solution)/shard_map/all_to_all | solution.py:28
  149.7 24.4 %all-to-all-done.3 = f32[32,2,8,512]{3,2,1,0:T(8,128)S(1)} async-done(((f32[32,2,8,512]{3,2,1,0:T(8,128)}), f32[32,2,8,512]{3,2,1,0:T(8,128)S(1)}, u32[]{:S(2)}, u32[]{:S(2)}) %all-to-all-start.3) | async-done | bytes 1048608 | tf_op jit(solution)/shard_map/all_to_all | solution.py:28
  174.1 1.7 reshape.178
  175.8 9.1 %gather_fusion = f32[2048,64]{1,0:T(8,128)} fusion(f32[4096,64]{1,0:T(8,128)} %reshape.178, s32[2048]{0:T(1024)S(1)} %broadcast_clamp_fusion), kind=kCustom, calls=%fused_computation | custom fusion | bytes 1056768 | tf_op jit(solution)/shard_map/jit(_take)/gather | solution.py:68
  185.0 2.4 %copy.40 = f32[16,128,64]{1,2,0:T(8,128)} copy(f32[16,128,64]{2,1,0:T(8,128)} %bitcast.68) | data formatting | bytes 1048576 | tf_op jit(solution)/shard_map/jit(_take)/gather | solution.py:68
  187.4 1.9 fusion.8
  189.7 1.9 fusion.7
  191.7 1.6 copy.41
  (37 shorter events, 6.7 us)
Async XLA Ops:
  7.2 7.2 %copy-start = (f32[16,128,256]{2,1,0:T(8,128)S(1)}, f32[16,128,256]{2,1,0:T(8,128)}, u32[]{:S(2)}) copy-start(f32[16,128,256]{2,1,0:T(8,128)} %param.10) | copy-start | bytes 6291460
  13.4 1.0 copy-start.2
  14.4 2.5 %copy-start.5 = (s32[16,128]{1,0:T(8,128)S(1)}, s32[16,128]{1,0:T(8,128)}, u32[]{:S(2)}) copy-start(s32[16,128]{1,0:T(8,128)} %param.11) | copy-start | bytes 24580
  32.1 15.4 %copy-start.6 = (f32[64,64]{1,0:T(8,128)S(1)}, f32[64,64]{1,0:T(8,128)}, u32[]{:S(2)}) copy-start(f32[64,64]{1,0:T(8,128)} %param.8) | copy-start | bytes 49156
  32.2 4.8 %collective-permute-start = (f32[32,8,512]{2,1,0:T(8,128)S(1)}, f32[32,8,512]{2,1,0:T(8,128)S(1)}, u32[]{:S(2)}, u32[]{:S(2)}) collective-permute-start(f32[32,8,512]{2,1,0:T(8,128)S(1)} %select_bitcast_fusion.1), channel_id=1, source_target_pairs={{0,4},{4,0},{1,5},{5,1},{2,6},{6,2},{3,7},{7,3},{8,12},{12,8},{9,1... | collective-permute-start | bytes 1572872 | tf_op jit(solution)/shard_map/ppermute | solution.py:16
  38.0 23.7 %all-to-all-start = ((f32[32,8,512]{2,1,0:T(8,128)}), f32[32,8,512]{2,1,0:T(8,128)S(1)}, u32[]{:S(2)}, u32[]{:S(2)}) async-start(f32[32,8,512]{2,1,0:T(8,128)} %fusion.13), calls=%async_computation | async-start | bytes 1048576 | tf_op jit(solution)/shard_map/all_to_all | solution.py:17
  61.9 4.4 %collective-permute-start.1 = (f32[8,512]{1,0:T(8,128)S(1)}, f32[8,512]{1,0:T(8,128)S(1)}, u32[]{:S(2)}, u32[]{:S(2)}) collective-permute-start(f32[8,512]{1,0:T(8,128)S(1)} %reshape.176), channel_id=1, source_target_pairs={{0,4},{4,0},{1,5},{5,1},{2,6},{6,2},{3,7},{7,3},{8,12},{12,8},{9,1... | collective-permute-start | bytes 49160 | tf_op jit(solution)/shard_map/ppermute | solution.py:25
  67.4 30.7 %all-to-all-start.1 = ((f32[32,2,8,512]{3,2,1,0:T(8,128)}), f32[32,2,8,512]{3,2,1,0:T(8,128)S(1)}, u32[]{:S(2)}, u32[]{:S(2)}) async-start(f32[32,2,8,512]{3,2,1,0:T(8,128)} %broadcast_in_dim.15), calls=%async_computation.1 | async-start | bytes 2097152 | tf_op jit(solution)/shard_map/all_to_all | solution.py:28
  72.8 28.6 %all-gather.2.cloned.1.call-start = ((), (), s32[]{:S(2)}) async-start(), calls=%async_computation.4 | async-start | bytes 1310720 | tf_op jit(solution)/shard_map/all_gather | solution.py:47
  101.5 3.8 %copy-start.4 = (f32[64,4096]{1,0:T(8,128)S(1)}, f32[64,4096]{1,0:T(8,128)}, u32[]{:S(2)}) copy-start(f32[64,4096]{1,0:T(8,128)} %all-gather.2.cloned.1.call-done) | copy-start | bytes 3145732
  109.7 4.5 %collective-permute-start.2 = (f32[32,8,512]{2,1,0:T(8,128)S(1)}, f32[32,8,512]{2,1,0:T(8,128)S(1)}, u32[]{:S(2)}, u32[]{:S(2)}) collective-permute-start(f32[32,8,512]{2,1,0:T(8,128)S(1)} %select_bitcast_fusion), channel_id=1, source_target_pairs={{0,4},{4,0},{1,5},{5,1},{2,6},{6,2},{3,7},{7,3},{8,12},{12,8},{9,1... | collective-permute-start | bytes 1572872 | tf_op jit(solution)/shard_map/ppermute | solution.py:16
  137.9 4.4 %collective-permute-start.3 = (f32[8,512]{1,0:T(8,128)S(1)}, f32[8,512]{1,0:T(8,128)S(1)}, u32[]{:S(2)}, u32[]{:S(2)}) collective-permute-start(f32[8,512]{1,0:T(8,128)S(1)} %reduce_sum.19), channel_id=1, source_target_pairs={{0,4},{4,0},{1,5},{5,1},{2,6},{6,2},{3,7},{7,3},{8,12},{12,8},{9,1... | collective-permute-start | bytes 49160 | tf_op jit(solution)/shard_map/ppermute | solution.py:25
  143.4 30.7 %all-to-all-start.3 = ((f32[32,2,8,512]{3,2,1,0:T(8,128)}), f32[32,2,8,512]{3,2,1,0:T(8,128)S(1)}, u32[]{:S(2)}, u32[]{:S(2)}) async-start(f32[32,2,8,512]{3,2,1,0:T(8,128)} %broadcast_in_dim.32), calls=%async_computation.3 | async-start | bytes 2097152 | tf_op jit(solution)/shard_map/all_to_all | solution.py:28
  185.0 2.4 %copy-start.3 = (f32[64,16,256]{2,0,1:T(8,128)S(1)}, f32[64,16,256]{2,0,1:T(8,128)}, u32[]{:S(2)}) copy-start(f32[64,16,256]{2,0,1:T(8,128)} %copy-done.2) | copy-start | bytes 3145732
  187.4 2.3 %copy-start.1 = (f32[16,256,256]{2,1,0:T(8,128)S(1)}, f32[16,256,256]{2,1,0:T(8,128)}, u32[]{:S(2)}) copy-start(f32[16,256,256]{2,1,0:T(8,128)} %param.9) | copy-start | bytes 12582916
Sparse Core Ops, SparseCore 0:
  75.5 25.9 all-gather.1

commit v3 on v1

--- a/solution.py
+++ b/solution.py
@@ -26,6 +26,19 @@
     return gathered.reshape(blocks * width, columns)
 
 
+def gather_columns(part):
+    count = lax.axis_size("rhs")
+    place = lax.axis_index("rhs")
+    shifted = [part] + [
+        lax.ppermute(part, "rhs", [(i, (i + step) % count) for i in range(count)])
+        for step in range(1, count)
+    ]
+    ahead = jnp.stack([shifted[(count - t) % count] for t in range(count)])
+    ordered = jnp.roll(ahead, place, axis=0)
+    rows, width = part.shape
+    return ordered.transpose(1, 0, 2).reshape(rows, count * width)
+
+
 def on_device(
     leaf_rhs, root_rhs, leaf_inverse, leaf_offdiagonal_block, update_rows, leaf_sizes, root_inverse
 ):
@@ -41,7 +54,7 @@
     update_terms = jnp.einsum(
         "dwu,wqu->wqd", leaf_forward_sweep, leaf_offdiagonal_block, precision=largest_entry
     )
-    root_full = lax.all_gather(root_inverse, "rhs", axis=1, tiled=True)
+    root_full = gather_columns(root_inverse)
     root_order = root_full.shape[1]
     width = root_rhs.shape[1]
     blocks = root_order // width

time: 203 us -> 185 us (0.911)
  between operations: 14.2 us -> 0.83 us
  waiting for transfers between devices: 73.4 us -> 62.8 us
  local copies, waits for them, and re-layouts: 28.4 us -> 34.6 us
  blocking collectives: 23.6 us -> 19.4 us
  starting transfers between devices: 32.5 us -> 35.7 us
    all_to_all x2, waiting for transfers between devices: 55.5 us -> 33.1 us  [share_all(): gathered = lax.all_to_all(copies, LEAF_AXES, 0, 0, tiled=False)]
    ppermute x0 -> x3, waiting for transfers between devices: none -> 12.2 us  [gather_columns(): lax.ppermute(part, 'rhs', [(i, (i + step) % count) for i in range(count)])]
    unnamed x17 -> x25, local copies, waits for them, and re-layouts: 3.79 us -> 10.1 us
    all_to_all x1, blocking collectives: 23.6 us -> 19.4 us  [owner_sum(): spread = lax.all_to_all(paired, ('y', 'z'), 0, 0, tiled=False)]
    ppermute x0 -> x3, starting transfers between devices: none -> 3.69 us  [gather_columns(): lax.ppermute(part, 'rhs', [(i, (i + step) % count) for i in range(count)])]
    dot_general x1, matrix products: 0.56 us -> 3.16 us  [on_device(): jnp.einsum('ic,ij->jc', forward_root, root_full, precision=largest_entry)]
  transfers between devices with their start and end apart: 6 -> 8, of which waited for: 5 -> 8; matrix products, arithmetic and copies ran while one was open for 1% -> 4% of each run, Pallas kernels for 0% -> 0%
where the time goes in v3:
time: 185 us
  waiting for transfers between devices  62.8 us (34%)
  starting transfers between devices  35.7 us (19%)
  local copies, waits for them, and re-layouts  34.6 us (19%)
  blocking collectives  19.4 us (10%)
  matrix products  15.9 us (9%)
  other arithmetic  15.5 us (8%)
    all_to_all x2, waiting for transfers between devices, share_all(): gathered = lax.all_to_all(copies, LEAF_AXES, 0, 0, tiled=False)  33.1 us
    all_to_all x1, blocking collectives, owner_sum(): spread = lax.all_to_all(paired, ('y', 'z'), 0, 0, tiled=False)  19.4 us
    all_to_all x2, starting transfers between devices, share_all(): gathered = lax.all_to_all(copies, LEAF_AXES, 0, 0, tiled=False)  19 us
    all_to_all x1, waiting for transfers between devices, owner_sum(): spread = lax.all_to_all(paired, ('y', 'z'), 0, 0, tiled=False)  14.1 us
    scatter-add x1, other arithmetic, on_device(): accumulated_sum = jnp.zeros((root_order, columns), jnp.float32).at[flat_r...  13.3 us
    ppermute x3, waiting for transfers between devices, gather_columns(): lax.ppermute(part, 'rhs', [(i, (i + step) % count) for i in range(count)])  12.2 us
    gather x2, local copies, waits for them, and re-layouts, on_device(): jnp.take(root_values, flat_rows, axis=0)  11.6 us
    unnamed x25, local copies, waits for them, and re-layouts  10.1 us
  transfers between devices with their start and end apart: 8, of which 8 were waited for; matrix products, arithmetic and copies ran while one was open for 4% of the time, Pallas kernels for 0%

profile of v3, /device:TPU:1, one launch (start us, length us, event | category | flops | bytes accessed | tf_op | source)
XLA Modules:
  0.0 184.6 jit_solution(7395845097875333094)
XLA Ops:
  1.5 5.3 %fusion.6 = f32[64,16,256]{2,0,1:T(8,128)S(1)} fusion(f32[16,256,256]{2,1,0:T(8,128)} %param.9, f32[16,256]{1,0:T(8,128)S(1)} %fusion.17, f32[64,16,256]{2,1,0:T(8,128)} %param.7), kind=kOutput, calls=%fused_computation.10 | convolution fusion | flops 404750336 | bytes 6307840 | tf_op jit(solution)/shard_map/clt,lst->cls/dot_general | solution.py:53
  7.9 1.2 convolution_bitcast_fusion.1
  9.1 1.3 copy.46
  10.4 13.3 %scatter_custom_fusion = f32[4096,64]{1,0:T(8,128)} fusion(s32[2048]{0:T(1024)S(1)} %bitcast.81, f32[2048,64]{1,0:T(8,128)} %bitcast.78, f32[]{:T(128)} %constant.51.clone.1), kind=kCustom, calls=%fused_computation.15 | custom fusion | flops 131072 | bytes 1049088 | tf_op jit(solution)/shard_map/scatter-add | solution.py:65
  23.7 1.9 %reshape_reshape.7 = f32[32,2,8,512]{3,2,1,0:T(8,128)S(1)} reshape(f32[4096,64]{1,0:T(8,128)} %scatter_custom_fusion) | data formatting | bytes 2097152 | tf_op jit(solution)/shard_map/reshape;reshape | solution.py:13
  25.7 3.3 %collective-permute-start.3 = (f32[32,8,512]{2,1,0:T(8,128)S(1)}, f32[32,8,512]{2,1,0:T(8,128)S(1)}, u32[]{:S(2)}, u32[]{:S(2)}) collective-permute-start(f32[32,8,512]{2,1,0:T(8,128)S(1)} %select_bitcast_fusion.1), channel_id=1, source_target_pairs={{0,4},{4,0},{1,5},{5,1},{2,6},{6,2},{3,7},{7,3},{8,12},{12,8},{9,1... | collective-permute-start | bytes 1572872 | tf_op jit(solution)/shard_map/ppermute | solution.py:16
  29.0 1.5 collective-permute-done.3
  31.5 9.5 %all-to-all-start = ((f32[32,8,512]{2,1,0:T(8,128)}), f32[32,8,512]{2,1,0:T(8,128)S(1)}, u32[]{:S(2)}, u32[]{:S(2)}) async-start(f32[32,8,512]{2,1,0:T(8,128)} %fusion.13), calls=%async_computation | async-start | bytes 1048576 | tf_op jit(solution)/shard_map/all_to_all | solution.py:17
  41.1 14.1 %all-to-all-done = f32[32,8,512]{2,1,0:T(8,128)S(1)} async-done(((f32[32,8,512]{2,1,0:T(8,128)}), f32[32,8,512]{2,1,0:T(8,128)S(1)}, u32[]{:S(2)}, u32[]{:S(2)}) %all-to-all-start) | async-done | bytes 524320 | tf_op jit(solution)/shard_map/all_to_all | solution.py:17
  55.4 1.1 broadcast_in_dim.32
  56.5 9.6 %all-to-all-start.1 = ((f32[64,8,512]{2,1,0:T(8,128)}), f32[64,8,512]{2,1,0:T(8,128)}, u32[]{:S(2)}, u32[]{:S(2)}) async-start(f32[64,8,512]{2,1,0:T(8,128)} %broadcast_in_dim.32), calls=%async_computation.1 | async-start | bytes 2097152 | tf_op jit(solution)/shard_map/all_to_all | solution.py:25
  66.1 2.6 %collective-permute-start = (f32[64,1024]{1,0:T(8,128)S(1)}, f32[64,1024]{1,0:T(8,128)S(1)}, u32[]{:S(2)}, u32[]{:S(2)}) collective-permute-start(f32[64,1024]{1,0:T(8,128)S(1)} %copy-done.4), channel_id=1, source_target_pairs={{0,3},{1,0},{2,1},{3,2},{4,7},{5,4},{6,5},{7,6},{8,11},{9,8},{10,9... | collective-permute-start | bytes 786440 | tf_op jit(solution)/shard_map/ppermute | solution.py:33
  70.5 4.1 %collective-permute-done = f32[64,1024]{1,0:T(8,128)S(1)} collective-permute-done((f32[64,1024]{1,0:T(8,128)S(1)}, f32[64,1024]{1,0:T(8,128)S(1)}, u32[]{:S(2)}, u32[]{:S(2)}) %collective-permute-start) | collective-permute-done | bytes 262176 | tf_op jit(solution)/shard_map/ppermute | solution.py:33
  75.3 2.1 %collective-permute-done.1 = f32[64,1024]{1,0:T(8,128)S(1)} collective-permute-done((f32[64,1024]{1,0:T(8,128)S(1)}, f32[64,1024]{1,0:T(8,128)S(1)}, u32[]{:S(2)}, u32[]{:S(2)}) %collective-permute-start.1) | collective-permute-done | bytes 262176 | tf_op jit(solution)/shard_map/ppermute | solution.py:33
  78.1 6.0 %collective-permute-done.2 = f32[64,1024]{1,0:T(8,128)S(1)} collective-permute-done((f32[64,1024]{1,0:T(8,128)S(1)}, f32[64,1024]{1,0:T(8,128)S(1)}, u32[]{:S(2)}, u32[]{:S(2)}) %collective-permute-start.2) | collective-permute-done | bytes 262176 | tf_op jit(solution)/shard_map/ppermute | solution.py:33
  87.7 1.3 dynamic-slice_bitcast_fusion
  89.1 5.4 %all-to-all-done.1 = f32[64,8,512]{2,1,0:T(8,128)} async-done(((f32[64,8,512]{2,1,0:T(8,128)}), f32[64,8,512]{2,1,0:T(8,128)}, u32[]{:S(2)}, u32[]{:S(2)}) %all-to-all-start.1) | async-done | bytes 1048608 | tf_op jit(solution)/shard_map/all_to_all | solution.py:25
  94.5 2.7 %reshape.114 = f32[4096,64]{1,0:T(8,128)} reshape(f32[64,8,512]{2,1,0:T(8,128)} %all-to-all-done.1) | data formatting | bytes 2097152 | tf_op jit(solution)/shard_map/reshape | solution.py:26
  97.3 2.4 %fusion.19 = f32[64,64]{1,0:T(8,128)S(1)} fusion(f32[64,4096]{1,0:T(8,128)S(1)} %bitcast.75, f32[4096,64]{1,0:T(8,128)} %reshape.114), kind=kOutput, calls=%fused_computation.45 | convolution fusion | flops 100663296 | bytes 2113536 | tf_op jit(solution)/shard_map/jc,ij->ic/dot_general | solution.py:69
  99.7 3.2 %fusion.20 = f32[4096,64]{1,0:T(8,128)} fusion(f32[64,4096]{1,0:T(8,128)S(1)} %bitcast.76, f32[64,64]{1,0:T(8,128)S(1)} %fusion.19), kind=kOutput, calls=%fused_computation.46 | convolution fusion | flops 100663296 | bytes 2113536 | tf_op jit(solution)/shard_map/ic,ij->jc/dot_general | solution.py:75
  102.8 1.9 %reshape_reshape.8 = f32[32,2,8,512]{3,2,1,0:T(8,128)S(1)} reshape(f32[4096,64]{1,0:T(8,128)} %fusion.20) | data formatting | bytes 2097152 | tf_op jit(solution)/shard_map/reshape;reshape | solution.py:13
  105.0 1.8 collective-permute-done.4
  107.0 19.4 %all_to_all.20 = f32[32,8,512]{2,1,0:T(8,128)S(1)} all-to-all(f32[32,8,512]{2,1,0:T(8,128)S(1)} %bitcast_add_fusion), channel_id=1, replica_groups=mesh['y'=4,'z'=8,'core'=2,'rhs'=4] {'y','z'}, dimensions={0} | all-to-all | bytes 1048576 | tf_op jit(solution)/shard_map/all_to_all | solution.py:17
  126.4 1.1 broadcast_in_dim.33
  127.5 9.4 %all-to-all-start.3 = ((f32[64,8,512]{2,1,0:T(8,128)}), f32[64,8,512]{2,1,0:T(8,128)S(1)}, u32[]{:S(2)}, u32[]{:S(2)}) async-start(f32[64,8,512]{2,1,0:T(8,128)} %broadcast_in_dim.33), calls=%async_computation.3 | async-start | bytes 2097152 | tf_op jit(solution)/shard_map/all_to_all | solution.py:25
  137.7 27.7 %all-to-all-done.3 = f32[64,8,512]{2,1,0:T(8,128)S(1)} async-done(((f32[64,8,512]{2,1,0:T(8,128)}), f32[64,8,512]{2,1,0:T(8,128)S(1)}, u32[]{:S(2)}, u32[]{:S(2)}) %all-to-all-start.3) | async-done | bytes 1048608 | tf_op jit(solution)/shard_map/all_to_all | solution.py:25
  165.4 1.8 reshape.115
  167.2 9.1 %gather_fusion = f32[2048,64]{1,0:T(8,128)} fusion(f32[4096,64]{1,0:T(8,128)} %reshape.115, s32[2048]{0:T(1024)S(1)} %broadcast_clamp_fusion), kind=kCustom, calls=%fused_computation | custom fusion | bytes 1056768 | tf_op jit(solution)/shard_map/jit(_take)/gather | solution.py:78
  176.4 2.4 %copy.42 = f32[16,128,64]{1,2,0:T(8,128)} copy(f32[16,128,64]{2,1,0:T(8,128)} %bitcast.77) | data formatting | bytes 1048576 | tf_op jit(solution)/shard_map/jit(_take)/gather | solution.py:78
  178.8 1.9 %fusion.8 = f32[64,16,256]{2,0,1:T(8,128)S(1)} fusion(f32[64,16,256]{2,0,1:T(8,128)S(1)} %copy-done.3, f32[16,128,256]{2,1,0:T(8,128)S(1)} %copy-done, f32[16,128,64]{1,2,0:T(8,128)} %copy.42, pred[16,128]{1,0:T(8,128)(4,1)S(1)} %compare_and_fusion), kind=kOutput, calls=%fused_computation.12 | convolution fusion | flops 201719808 | bytes 4720640 | tf_op jit(solution)/shard_map/nvr,nvb->rnb/dot_general | solution.py:79
  181.1 1.9 %fusion.7 = f32[64,16,256]{2,0,1:T(8,128)S(1)} fusion(f32[64,16,256]{2,0,1:T(8,128)S(1)} %fusion.8, f32[16,256,256]{2,1,0:T(8,128)S(1)} %copy-done.1, f32[16,256]{1,0:T(8,128)S(1)} %fusion.17), kind=kOutput, calls=%fused_computation.11 | convolution fusion | flops 404750336 | bytes 6307840 | tf_op jit(solution)/shard_map/cls,lst->clt/dot_general | solution.py:82
  183.0 1.6 copy.43
  (42 shorter events, 11.8 us)
Async XLA Ops:
  0.6 7.2 %copy-start = (f32[16,128,256]{2,1,0:T(8,128)S(1)}, f32[16,128,256]{2,1,0:T(8,128)}, u32[]{:S(2)}) copy-start(f32[16,128,256]{2,1,0:T(8,128)} %param.10) | copy-start | bytes 6291460
  6.9 1.0 copy-start.2
  7.9 2.5 %copy-start.5 = (s32[16,128]{1,0:T(8,128)S(1)}, s32[16,128]{1,0:T(8,128)}, u32[]{:S(2)}) copy-start(s32[16,128]{1,0:T(8,128)} %param.11) | copy-start | bytes 24580
  25.6 15.4 %copy-start.6 = (f32[64,64]{1,0:T(8,128)S(1)}, f32[64,64]{1,0:T(8,128)}, u32[]{:S(2)}) copy-start(f32[64,64]{1,0:T(8,128)} %param.8) | copy-start | bytes 49156
  25.7 4.8 %collective-permute-start.3 = (f32[32,8,512]{2,1,0:T(8,128)S(1)}, f32[32,8,512]{2,1,0:T(8,128)S(1)}, u32[]{:S(2)}, u32[]{:S(2)}) collective-permute-start(f32[32,8,512]{2,1,0:T(8,128)S(1)} %select_bitcast_fusion.1), channel_id=1, source_target_pairs={{0,4},{4,0},{1,5},{5,1},{2,6},{6,2},{3,7},{7,3},{8,12},{12,8},{9,1... | collective-permute-start | bytes 1572872 | tf_op jit(solution)/shard_map/ppermute | solution.py:16
  31.5 23.7 %all-to-all-start = ((f32[32,8,512]{2,1,0:T(8,128)}), f32[32,8,512]{2,1,0:T(8,128)S(1)}, u32[]{:S(2)}, u32[]{:S(2)}) async-start(f32[32,8,512]{2,1,0:T(8,128)} %fusion.13), calls=%async_computation | async-start | bytes 1048576 | tf_op jit(solution)/shard_map/all_to_all | solution.py:17
  41.0 25.1 %copy-start.4 = (f32[64,1024]{1,0:T(8,128)S(1)}, f32[64,1024]{1,0:T(8,128)}, u32[]{:S(2)}) copy-start(f32[64,1024]{1,0:T(8,128)} %param.13) | copy-start | bytes 786436
  56.5 38.1 %all-to-all-start.1 = ((f32[64,8,512]{2,1,0:T(8,128)}), f32[64,8,512]{2,1,0:T(8,128)}, u32[]{:S(2)}, u32[]{:S(2)}) async-start(f32[64,8,512]{2,1,0:T(8,128)} %broadcast_in_dim.32), calls=%async_computation.1 | async-start | bytes 2097152 | tf_op jit(solution)/shard_map/all_to_all | solution.py:25
  66.1 8.5 %collective-permute-start = (f32[64,1024]{1,0:T(8,128)S(1)}, f32[64,1024]{1,0:T(8,128)S(1)}, u32[]{:S(2)}, u32[]{:S(2)}) collective-permute-start(f32[64,1024]{1,0:T(8,128)S(1)} %copy-done.4), channel_id=1, source_target_pairs={{0,3},{1,0},{2,1},{3,2},{4,7},{5,4},{6,5},{7,6},{8,11},{9,8},{10,9... | collective-permute-start | bytes 786440 | tf_op jit(solution)/shard_map/ppermute | solution.py:33
  68.7 8.7 %collective-permute-start.1 = (f32[64,1024]{1,0:T(8,128)S(1)}, f32[64,1024]{1,0:T(8,128)S(1)}, u32[]{:S(2)}, u32[]{:S(2)}) collective-permute-start(f32[64,1024]{1,0:T(8,128)S(1)} %copy-done.4), channel_id=1, source_target_pairs={{0,2},{1,3},{2,0},{3,1},{4,6},{5,7},{6,4},{7,5},{8,10},{9,11},{10,... | collective-permute-start | bytes 786440 | tf_op jit(solution)/shard_map/ppermute | solution.py:33
  69.2 14.9 %collective-permute-start.2 = (f32[64,1024]{1,0:T(8,128)S(1)}, f32[64,1024]{1,0:T(8,128)S(1)}, u32[]{:S(2)}, u32[]{:S(2)}) collective-permute-start(f32[64,1024]{1,0:T(8,128)S(1)} %copy-done.4), channel_id=1, source_target_pairs={{0,1},{1,2},{2,3},{3,0},{4,5},{5,6},{6,7},{7,4},{8,9},{9,10},{10,1... | collective-permute-start | bytes 786440 | tf_op jit(solution)/shard_map/ppermute | solution.py:33
  104.8 2.0 %collective-permute-start.4 = (f32[32,8,512]{2,1,0:T(8,128)S(1)}, f32[32,8,512]{2,1,0:T(8,128)S(1)}, u32[]{:S(2)}, u32[]{:S(2)}) collective-permute-start(f32[32,8,512]{2,1,0:T(8,128)S(1)} %select_bitcast_fusion), channel_id=1, source_target_pairs={{0,4},{4,0},{1,5},{5,1},{2,6},{6,2},{3,7},{7,3},{8,12},{12,8},{9,1... | collective-permute-start | bytes 1572872 | tf_op jit(solution)/shard_map/ppermute | solution.py:16
  127.5 37.9 %all-to-all-start.3 = ((f32[64,8,512]{2,1,0:T(8,128)}), f32[64,8,512]{2,1,0:T(8,128)S(1)}, u32[]{:S(2)}, u32[]{:S(2)}) async-start(f32[64,8,512]{2,1,0:T(8,128)} %broadcast_in_dim.33), calls=%async_computation.3 | async-start | bytes 2097152 | tf_op jit(solution)/shard_map/all_to_all | solution.py:25
  176.3 2.4 %copy-start.3 = (f32[64,16,256]{2,0,1:T(8,128)S(1)}, f32[64,16,256]{2,0,1:T(8,128)}, u32[]{:S(2)}) copy-start(f32[64,16,256]{2,0,1:T(8,128)} %copy-done.2) | copy-start | bytes 3145732
  178.8 2.3 %copy-start.1 = (f32[16,256,256]{2,1,0:T(8,128)S(1)}, f32[16,256,256]{2,1,0:T(8,128)}, u32[]{:S(2)}) copy-start(f32[16,256,256]{2,1,0:T(8,128)} %param.9) | copy-start | bytes 12582916

commit v4 on v3

--- a/solution.py
+++ b/solution.py
@@ -1,10 +1,46 @@
 import jax
 import jax.numpy as jnp
 from jax import lax
+from jax.experimental import pallas as pl
+from jax.experimental.pallas import tpu as pltpu
 from jax.sharding import Mesh
 from jax.sharding import PartitionSpec as P
 
 LEAF_AXES = ("y", "z", "core")
+
+
+GROUP = 8
+
+
+def scatter_rows(rows, updates, order):
+    count, columns = updates.shape
+
+    def kernel(rows_ref, upd_ref, out_ref):
+        out_ref[...] = jnp.zeros_like(out_ref)
+
+        def body(group, carry):
+            base = group * GROUP
+            targets = [rows_ref[base + u] for u in range(GROUP)]
+            sums = [
+                out_ref[pl.ds(targets[u], 1), :] + upd_ref[pl.ds(base + u, 1), :]
+                for u in range(GROUP)
+            ]
+            for u in range(GROUP):
+                out_ref[pl.ds(targets[u], 1), :] = sums[u]
+            return carry
+
+        lax.fori_loop(0, count // GROUP, body, 0)
+
+    return pl.pallas_call(
+        kernel,
+        out_shape=jax.ShapeDtypeStruct((order, columns), jnp.float32),
+        grid_spec=pltpu.PrefetchScalarGridSpec(
+            num_scalar_prefetch=1,
+            grid=(1,),
+            in_specs=[pl.BlockSpec((count, columns), lambda i, r: (0, 0))],
+            out_specs=pl.BlockSpec((order, columns), lambda i, r: (0, 0)),
+        ),
+    )(rows, updates)
 
 
 def owner_sum(parts):
@@ -59,10 +95,9 @@
     width = root_rhs.shape[1]
     blocks = root_order // width
     flat_rows = update_rows.reshape(-1)
-    accumulated_sum = (
-        jnp.zeros((root_order, columns), jnp.float32)
-        .at[flat_rows]
-        .add(update_terms.reshape(leaf_count * touched, columns))
+    assert touched % GROUP == 0
+    accumulated_sum = scatter_rows(
+        flat_rows, update_terms.reshape(leaf_count * touched, columns), root_order
     )
     shares = owner_sum(accumulated_sum.reshape(blocks, width, columns))
     reduced = root_rhs.T - shares

time: 185 us -> 177 us (0.957)
  other arithmetic: 15.5 us -> 2.26 us
  Pallas kernels: 0 us -> 7.11 us
  local copies, waits for them, and re-layouts: 34.6 us -> 32 us
    scatter-add x1 -> x0, other arithmetic: 13.3 us -> none  [on_device(): accumulated_sum = jnp.zeros((root_order, columns), jnp.float32).at[flat_r...]
    pallas_call x0 -> x1, Pallas kernels: none -> 7.11 us  [scatter_rows(): pl.pallas_call(kernel, out_shape=jax.ShapeDtypeStruct((order, columns), j...]
    gather x2 -> x1, local copies, waits for them, and re-layouts: 11.6 us -> 9.29 us  [on_device(): jnp.take(root_values, flat_rows, axis=0)]
  transfers between devices with their start and end apart: 8 -> 8, of which waited for: 8 -> 8; matrix products, arithmetic and copies ran while one was open for 4% -> 5% of each run, Pallas kernels for 0% -> 0%
where the time goes in v4:
time: 177 us
  waiting for transfers between devices  62.6 us (35%)
  starting transfers between devices  35.7 us (20%)
  local copies, waits for them, and re-layouts  32 us (18%)
  blocking collectives  19.4 us (11%)
  matrix products  16.7 us (9%)
  Pallas kernels  7.11 us (4%)
  other arithmetic  2.26 us (1%)
    all_to_all x2, waiting for transfers between devices, share_all(): gathered = lax.all_to_all(copies, LEAF_AXES, 0, 0, tiled=False)  33 us
    all_to_all x1, blocking collectives, owner_sum(): spread = lax.all_to_all(paired, ('y', 'z'), 0, 0, tiled=False)  19.4 us
    all_to_all x2, starting transfers between devices, share_all(): gathered = lax.all_to_all(copies, LEAF_AXES, 0, 0, tiled=False)  19 us
    all_to_all x1, waiting for transfers between devices, owner_sum(): spread = lax.all_to_all(paired, ('y', 'z'), 0, 0, tiled=False)  14.1 us
    ppermute x3, waiting for transfers between devices, gather_columns(): lax.ppermute(part, 'rhs', [(i, (i + step) % count) for i in range(count)])  12.2 us
    unnamed x25, local copies, waits for them, and re-layouts  9.76 us
    all_to_all x1, starting transfers between devices, owner_sum(): spread = lax.all_to_all(paired, ('y', 'z'), 0, 0, tiled=False)  9.5 us
    gather x1, local copies, waits for them, and re-layouts, on_device(): jnp.take(root_values, flat_rows, axis=0)  9.29 us
  transfers between devices with their start and end apart: 8, of which 8 were waited for; matrix products, arithmetic and copies ran while one was open for 5% of the time, Pallas kernels for 0%

profile of v4, /device:TPU:1, one launch (start us, length us, event | category | flops | bytes accessed | tf_op | source)
XLA Modules:
  0.0 176.6 jit_solution(1613977254869193189)
XLA Ops:
  1.5 5.3 %fusion.6 = f32[64,16,256]{2,0,1:T(8,128)S(1)} fusion(f32[16,256,256]{2,1,0:T(8,128)} %param.9, f32[16,256]{1,0:T(8,128)S(1)} %fusion.15, f32[64,16,256]{2,1,0:T(8,128)} %param.7), kind=kOutput, calls=%fused_computation.8 | convolution fusion | flops 404750336 | bytes 6307840 | tf_op jit(solution)/shard_map/clt,lst->cls/dot_general | solution.py:89
  6.9 1.0 copy-done.2
  7.9 1.2 convolution_bitcast_fusion.1
  9.1 1.3 copy.19
  10.4 7.1 %shard_map.86 = f32[4096,64]{1,0:T(8,128)} custom-call(s32[2048]{0:T(1024)} %bitcast.81, f32[2048,64]{1,0:T(8,128)} %bitcast.78), custom_call_target="tpu_custom_call" | custom-call | tf_op jit(solution)/shard_map/pallas_call | solution.py:34
  17.5 1.9 %reshape_reshape.7 = f32[32,2,8,512]{3,2,1,0:T(8,128)S(1)} reshape(f32[4096,64]{1,0:T(8,128)} %shard_map.86) | data formatting | bytes 2097152 | tf_op jit(solution)/shard_map/reshape;reshape | solution.py:49
  19.5 3.3 %collective-permute-start.3 = (f32[32,8,512]{2,1,0:T(8,128)S(1)}, f32[32,8,512]{2,1,0:T(8,128)S(1)}, u32[]{:S(2)}, u32[]{:S(2)}) collective-permute-start(f32[32,8,512]{2,1,0:T(8,128)S(1)} %select_bitcast_fusion.1), channel_id=1, source_target_pairs={{0,4},{4,0},{1,5},{5,1},{2,6},{6,2},{3,7},{7,3},{8,12},{12,8},{9,1... | collective-permute-start | bytes 1572872 | tf_op jit(solution)/shard_map/ppermute | solution.py:52
  22.8 1.5 collective-permute-done.3
  25.3 9.5 %all-to-all-start = ((f32[32,8,512]{2,1,0:T(8,128)}), f32[32,8,512]{2,1,0:T(8,128)S(1)}, u32[]{:S(2)}, u32[]{:S(2)}) async-start(f32[32,8,512]{2,1,0:T(8,128)} %fusion.12), calls=%async_computation | async-start | bytes 1048576 | tf_op jit(solution)/shard_map/all_to_all | solution.py:53
  34.9 14.1 %all-to-all-done = f32[32,8,512]{2,1,0:T(8,128)S(1)} async-done(((f32[32,8,512]{2,1,0:T(8,128)}), f32[32,8,512]{2,1,0:T(8,128)S(1)}, u32[]{:S(2)}, u32[]{:S(2)}) %all-to-all-start) | async-done | bytes 524320 | tf_op jit(solution)/shard_map/all_to_all | solution.py:53
  49.2 1.1 broadcast_in_dim.27
  50.3 9.6 %all-to-all-start.1 = ((f32[64,8,512]{2,1,0:T(8,128)}), f32[64,8,512]{2,1,0:T(8,128)}, u32[]{:S(2)}, u32[]{:S(2)}) async-start(f32[64,8,512]{2,1,0:T(8,128)} %broadcast_in_dim.27), calls=%async_computation.1 | async-start | bytes 2097152 | tf_op jit(solution)/shard_map/all_to_all | solution.py:61
  60.0 2.6 %collective-permute-start = (f32[64,1024]{1,0:T(8,128)S(1)}, f32[64,1024]{1,0:T(8,128)S(1)}, u32[]{:S(2)}, u32[]{:S(2)}) collective-permute-start(f32[64,1024]{1,0:T(8,128)S(1)} %copy-done.4), channel_id=1, source_target_pairs={{0,3},{1,0},{2,1},{3,2},{4,7},{5,4},{6,5},{7,6},{8,11},{9,8},{10,9... | collective-permute-start | bytes 786440 | tf_op jit(solution)/shard_map/ppermute | solution.py:69
  64.4 4.1 %collective-permute-done = f32[64,1024]{1,0:T(8,128)S(1)} collective-permute-done((f32[64,1024]{1,0:T(8,128)S(1)}, f32[64,1024]{1,0:T(8,128)S(1)}, u32[]{:S(2)}, u32[]{:S(2)}) %collective-permute-start) | collective-permute-done | bytes 262176 | tf_op jit(solution)/shard_map/ppermute | solution.py:69
  69.2 2.0 %collective-permute-done.1 = f32[64,1024]{1,0:T(8,128)S(1)} collective-permute-done((f32[64,1024]{1,0:T(8,128)S(1)}, f32[64,1024]{1,0:T(8,128)S(1)}, u32[]{:S(2)}, u32[]{:S(2)}) %collective-permute-start.1) | collective-permute-done | bytes 262176 | tf_op jit(solution)/shard_map/ppermute | solution.py:69
  71.9 6.0 %collective-permute-done.2 = f32[64,1024]{1,0:T(8,128)S(1)} collective-permute-done((f32[64,1024]{1,0:T(8,128)S(1)}, f32[64,1024]{1,0:T(8,128)S(1)}, u32[]{:S(2)}, u32[]{:S(2)}) %collective-permute-start.2) | collective-permute-done | bytes 262176 | tf_op jit(solution)/shard_map/ppermute | solution.py:69
  81.6 1.3 dynamic-slice_bitcast_fusion
  83.1 5.3 %all-to-all-done.1 = f32[64,8,512]{2,1,0:T(8,128)} async-done(((f32[64,8,512]{2,1,0:T(8,128)}), f32[64,8,512]{2,1,0:T(8,128)}, u32[]{:S(2)}, u32[]{:S(2)}) %all-to-all-start.1) | async-done | bytes 1048608 | tf_op jit(solution)/shard_map/all_to_all | solution.py:61
  88.4 2.7 %reshape.116 = f32[4096,64]{1,0:T(8,128)} reshape(f32[64,8,512]{2,1,0:T(8,128)} %all-to-all-done.1) | data formatting | bytes 2097152 | tf_op jit(solution)/shard_map/reshape | solution.py:62
  91.1 2.4 %fusion.17 = f32[64,64]{1,0:T(8,128)S(1)} fusion(f32[64,4096]{1,0:T(8,128)S(1)} %bitcast.76, f32[4096,64]{1,0:T(8,128)} %reshape.116), kind=kOutput, calls=%fused_computation.42 | convolution fusion | flops 100663296 | bytes 2113536 | tf_op jit(solution)/shard_map/jc,ij->ic/dot_general | solution.py:104
  93.5 3.1 %fusion.18 = f32[4096,64]{1,0:T(8,128)} fusion(f32[64,4096]{1,0:T(8,128)S(1)} %bitcast.77, f32[64,64]{1,0:T(8,128)S(1)} %fusion.17), kind=kOutput, calls=%fused_computation.43 | convolution fusion | flops 100663296 | bytes 2113536 | tf_op jit(solution)/shard_map/ic,ij->jc/dot_general | solution.py:110
  96.6 1.9 %reshape_reshape.8 = f32[32,2,8,512]{3,2,1,0:T(8,128)S(1)} reshape(f32[4096,64]{1,0:T(8,128)} %fusion.18) | data formatting | bytes 2097152 | tf_op jit(solution)/shard_map/reshape;reshape | solution.py:49
  98.8 1.8 %collective-permute-done.4 = f32[32,8,512]{2,1,0:T(8,128)S(1)} collective-permute-done((f32[32,8,512]{2,1,0:T(8,128)S(1)}, f32[32,8,512]{2,1,0:T(8,128)S(1)}, u32[]{:S(2)}, u32[]{:S(2)}) %collective-permute-start.4) | collective-permute-done | bytes 524320 | tf_op jit(solution)/shard_map/ppermute | solution.py:52
  100.8 19.4 %all_to_all.20 = f32[32,8,512]{2,1,0:T(8,128)S(1)} all-to-all(f32[32,8,512]{2,1,0:T(8,128)S(1)} %bitcast_add_fusion), channel_id=1, replica_groups=mesh['y'=4,'z'=8,'core'=2,'rhs'=4] {'y','z'}, dimensions={0} | all-to-all | bytes 1048576 | tf_op jit(solution)/shard_map/all_to_all | solution.py:53
  120.2 1.1 broadcast_in_dim.28
  121.3 9.4 %all-to-all-start.3 = ((f32[64,8,512]{2,1,0:T(8,128)}), f32[64,8,512]{2,1,0:T(8,128)S(1)}, u32[]{:S(2)}, u32[]{:S(2)}) async-start(f32[64,8,512]{2,1,0:T(8,128)} %broadcast_in_dim.28), calls=%async_computation.3 | async-start | bytes 2097152 | tf_op jit(solution)/shard_map/all_to_all | solution.py:61
  131.6 27.7 %all-to-all-done.3 = f32[64,8,512]{2,1,0:T(8,128)S(1)} async-done(((f32[64,8,512]{2,1,0:T(8,128)}), f32[64,8,512]{2,1,0:T(8,128)S(1)}, u32[]{:S(2)}, u32[]{:S(2)}) %all-to-all-start.3) | async-done | bytes 1048608 | tf_op jit(solution)/shard_map/all_to_all | solution.py:61
  159.3 1.8 reshape.117
  161.0 9.3 %gather_fusion = f32[2048,64]{1,0:T(8,128)} fusion(f32[4096,64]{1,0:T(8,128)} %reshape.117, s32[2048]{0:T(1024)S(1)} %broadcast_clamp_fusion), kind=kCustom, calls=%fused_computation | custom fusion | bytes 1056768 | tf_op jit(solution)/shard_map/jit(_take)/gather | solution.py:113
  170.3 2.7 %fusion.8 = f32[64,16,256]{2,0,1:T(8,128)S(1)} fusion(f32[64,16,256]{2,0,1:T(8,128)S(1)} %copy-done.3, f32[16,128,256]{2,1,0:T(8,128)S(1)} %copy-done, f32[16,128,64]{2,1,0:T(8,128)} %bitcast.79, pred[16,128]{1,0:T(8,128)(4,1)S(1)} %compare_and_fusion), kind=kOutput, calls=%fused_computation.11 | convolution fusion | flops 201719808 | bytes 4720640 | tf_op jit(solution)/shard_map/nvr,nvb->rnb/dot_general | solution.py:114
  173.1 1.9 %fusion.7 = f32[64,16,256]{2,0,1:T(8,128)S(1)} fusion(f32[64,16,256]{2,0,1:T(8,128)S(1)} %fusion.8, f32[16,256,256]{2,1,0:T(8,128)S(1)} %copy-done.1, f32[16,256]{1,0:T(8,128)S(1)} %fusion.15), kind=kOutput, calls=%fused_computation.9 | convolution fusion | flops 404750336 | bytes 6307840 | tf_op jit(solution)/shard_map/cls,lst->clt/dot_general | solution.py:117
  175.0 1.6 copy.27
  (41 shorter events, 10.5 us)
Async XLA Ops:
  0.6 7.2 %copy-start = (f32[16,128,256]{2,1,0:T(8,128)S(1)}, f32[16,128,256]{2,1,0:T(8,128)}, u32[]{:S(2)}) copy-start(f32[16,128,256]{2,1,0:T(8,128)} %param.10) | copy-start | bytes 6291460
  6.9 1.0 copy-start.2
  19.4 15.4 %copy-start.6 = (f32[64,64]{1,0:T(8,128)S(1)}, f32[64,64]{1,0:T(8,128)}, u32[]{:S(2)}) copy-start(f32[64,64]{1,0:T(8,128)} %param.8) | copy-start | bytes 49156
  19.5 4.8 %collective-permute-start.3 = (f32[32,8,512]{2,1,0:T(8,128)S(1)}, f32[32,8,512]{2,1,0:T(8,128)S(1)}, u32[]{:S(2)}, u32[]{:S(2)}) collective-permute-start(f32[32,8,512]{2,1,0:T(8,128)S(1)} %select_bitcast_fusion.1), channel_id=1, source_target_pairs={{0,4},{4,0},{1,5},{5,1},{2,6},{6,2},{3,7},{7,3},{8,12},{12,8},{9,1... | collective-permute-start | bytes 1572872 | tf_op jit(solution)/shard_map/ppermute | solution.py:52
  25.3 23.7 %all-to-all-start = ((f32[32,8,512]{2,1,0:T(8,128)}), f32[32,8,512]{2,1,0:T(8,128)S(1)}, u32[]{:S(2)}, u32[]{:S(2)}) async-start(f32[32,8,512]{2,1,0:T(8,128)} %fusion.12), calls=%async_computation | async-start | bytes 1048576 | tf_op jit(solution)/shard_map/all_to_all | solution.py:53
  34.8 25.1 %copy-start.4 = (f32[64,1024]{1,0:T(8,128)S(1)}, f32[64,1024]{1,0:T(8,128)}, u32[]{:S(2)}) copy-start(f32[64,1024]{1,0:T(8,128)} %param.13) | copy-start | bytes 786436
  50.3 38.1 %all-to-all-start.1 = ((f32[64,8,512]{2,1,0:T(8,128)}), f32[64,8,512]{2,1,0:T(8,128)}, u32[]{:S(2)}, u32[]{:S(2)}) async-start(f32[64,8,512]{2,1,0:T(8,128)} %broadcast_in_dim.27), calls=%async_computation.1 | async-start | bytes 2097152 | tf_op jit(solution)/shard_map/all_to_all | solution.py:61
  60.0 8.5 %collective-permute-start = (f32[64,1024]{1,0:T(8,128)S(1)}, f32[64,1024]{1,0:T(8,128)S(1)}, u32[]{:S(2)}, u32[]{:S(2)}) collective-permute-start(f32[64,1024]{1,0:T(8,128)S(1)} %copy-done.4), channel_id=1, source_target_pairs={{0,3},{1,0},{2,1},{3,2},{4,7},{5,4},{6,5},{7,6},{8,11},{9,8},{10,9... | collective-permute-start | bytes 786440 | tf_op jit(solution)/shard_map/ppermute | solution.py:69
  62.5 8.7 %collective-permute-start.1 = (f32[64,1024]{1,0:T(8,128)S(1)}, f32[64,1024]{1,0:T(8,128)S(1)}, u32[]{:S(2)}, u32[]{:S(2)}) collective-permute-start(f32[64,1024]{1,0:T(8,128)S(1)} %copy-done.4), channel_id=1, source_target_pairs={{0,2},{1,3},{2,0},{3,1},{4,6},{5,7},{6,4},{7,5},{8,10},{9,11},{10,... | collective-permute-start | bytes 786440 | tf_op jit(solution)/shard_map/ppermute | solution.py:69
  63.0 14.9 %collective-permute-start.2 = (f32[64,1024]{1,0:T(8,128)S(1)}, f32[64,1024]{1,0:T(8,128)S(1)}, u32[]{:S(2)}, u32[]{:S(2)}) collective-permute-start(f32[64,1024]{1,0:T(8,128)S(1)} %copy-done.4), channel_id=1, source_target_pairs={{0,1},{1,2},{2,3},{3,0},{4,5},{5,6},{6,7},{7,4},{8,9},{9,10},{10,1... | collective-permute-start | bytes 786440 | tf_op jit(solution)/shard_map/ppermute | solution.py:69
  98.7 2.0 %collective-permute-start.4 = (f32[32,8,512]{2,1,0:T(8,128)S(1)}, f32[32,8,512]{2,1,0:T(8,128)S(1)}, u32[]{:S(2)}, u32[]{:S(2)}) collective-permute-start(f32[32,8,512]{2,1,0:T(8,128)S(1)} %select_bitcast_fusion), channel_id=1, source_target_pairs={{0,4},{4,0},{1,5},{5,1},{2,6},{6,2},{3,7},{7,3},{8,12},{12,8},{9,1... | collective-permute-start | bytes 1572872 | tf_op jit(solution)/shard_map/ppermute | solution.py:52
  120.2 10.6 %copy-start.5 = (s32[16,128]{1,0:T(8,128)S(1)}, s32[16,128]{1,0:T(8,128)}, u32[]{:S(2)}) copy-start(s32[16,128]{1,0:T(8,128)} %param.11) | copy-start | bytes 24580
  121.3 37.9 %all-to-all-start.3 = ((f32[64,8,512]{2,1,0:T(8,128)}), f32[64,8,512]{2,1,0:T(8,128)S(1)}, u32[]{:S(2)}, u32[]{:S(2)}) async-start(f32[64,8,512]{2,1,0:T(8,128)} %broadcast_in_dim.28), calls=%async_computation.3 | async-start | bytes 2097152 | tf_op jit(solution)/shard_map/all_to_all | solution.py:61
  161.0 9.3 %copy-start.3 = (f32[64,16,256]{2,0,1:T(8,128)S(1)}, f32[64,16,256]{2,0,1:T(8,128)}, u32[]{:S(2)}) copy-start(f32[64,16,256]{2,0,1:T(8,128)} %copy-done.2) | copy-start | bytes 3145732
  170.3 2.7 %copy-start.1 = (f32[16,256,256]{2,1,0:T(8,128)S(1)}, f32[16,256,256]{2,1,0:T(8,128)}, u32[]{:S(2)}) copy-start(f32[16,256,256]{2,1,0:T(8,128)} %param.9) | copy-start | bytes 12582916

commit v5 on v4

--- a/solution.py
+++ b/solution.py
@@ -9,7 +9,7 @@
 LEAF_AXES = ("y", "z", "core")
 
 
-GROUP = 8
+GROUP = 16
 
 
 def scatter_rows(rows, updates, order):
@@ -41,6 +41,32 @@
             out_specs=pl.BlockSpec((order, columns), lambda i, r: (0, 0)),
         ),
     )(rows, updates)
+
+
+def gather_rows(rows, table):
+    count = rows.shape[0]
+    order, columns = table.shape
+
+    def kernel(rows_ref, table_ref, out_ref):
+        def body(group, carry):
+            base = group * GROUP
+            picked = [table_ref[pl.ds(rows_ref[base + u], 1), :] for u in range(GROUP)]
+            for u in range(GROUP):
+                out_ref[pl.ds(base + u, 1), :] = picked[u]
+            return carry
+
+        lax.fori_loop(0, count // GROUP, body, 0)
+
+    return pl.pallas_call(
+        kernel,
+        out_shape=jax.ShapeDtypeStruct((count, columns), jnp.float32),
+        grid_spec=pltpu.PrefetchScalarGridSpec(
+            num_scalar_prefetch=1,
+            grid=(1,),
+            in_specs=[pl.BlockSpec((order, columns), lambda i, r: (0, 0))],
+            out_specs=pl.BlockSpec((count, columns), lambda i, r: (0, 0)),
+        ),
+    )(rows, table)
 
 
 def owner_sum(parts):
@@ -110,7 +136,7 @@
     back_terms = jnp.einsum("ic,ij->jc", forward_root, root_full, precision=largest_entry)
     root_solution = owner_sum(back_terms.reshape(blocks, width, columns))
     root_values = share_all(root_solution, blocks)
-    selected_rows = jnp.take(root_values, flat_rows, axis=0).reshape(leaf_count, touched, columns)
+    selected_rows = gather_rows(flat_rows, root_values).reshape(leaf_count, touched, columns)
     adjusted_values = leaf_forward_sweep - jnp.einsum(
         "nvr,nvb->rnb", selected_rows, leaf_offdiagonal_block, precision=largest_entry
     )

time: 177 us -> 173 us (0.977)
  local copies, waits for them, and re-layouts: 32 us -> 22.6 us
  Pallas kernels: 7.11 us -> 12.4 us
    gather x1 -> x0, local copies, waits for them, and re-layouts: 9.29 us -> none  [on_device(): jnp.take(root_values, flat_rows, axis=0)]
    pallas_call x0 -> x1, Pallas kernels: none -> 5.71 us  [gather_rows(): pl.pallas_call(kernel, out_shape=jax.ShapeDtypeStruct((count, columns), j...]
    unnamed x25 -> x23, local copies, waits for them, and re-layouts: 9.76 us -> 9.7 us
where the time goes in v5:
time: 173 us; the launch traced here: 172 us
  waiting for transfers between devices  62.8 us (36%)
  starting transfers between devices  35.7 us (21%)
  local copies, waits for them, and re-layouts  22.6 us (13%)
  blocking collectives  19.4 us (11%)
  matrix products  16.6 us (10%)
  Pallas kernels  12.4 us (7%)
  other arithmetic  2.22 us (1%)
    all_to_all x2, waiting for transfers between devices, share_all(): gathered = lax.all_to_all(copies, LEAF_AXES, 0, 0, tiled=False)  33.1 us
    all_to_all x1, blocking collectives, owner_sum(): spread = lax.all_to_all(paired, ('y', 'z'), 0, 0, tiled=False)  19.4 us
    all_to_all x2, starting transfers between devices, share_all(): gathered = lax.all_to_all(copies, LEAF_AXES, 0, 0, tiled=False)  19 us
    all_to_all x1, waiting for transfers between devices, owner_sum(): spread = lax.all_to_all(paired, ('y', 'z'), 0, 0, tiled=False)  14.1 us
    ppermute x3, waiting for transfers between devices, gather_columns(): lax.ppermute(part, 'rhs', [(i, (i + step) % count) for i in range(count)])  12.2 us
    unnamed x23, local copies, waits for them, and re-layouts  9.7 us
    all_to_all x1, starting transfers between devices, owner_sum(): spread = lax.all_to_all(paired, ('y', 'z'), 0, 0, tiled=False)  9.49 us
    pallas_call x1, Pallas kernels, scatter_rows(): pl.pallas_call(kernel, out_shape=jax.ShapeDtypeStruct((order, columns), j...  6.7 us
  transfers between devices with their start and end apart: 8, of which 8 were waited for; matrix products, arithmetic and copies ran while one was open for 5% of the time, Pallas kernels for 0%

profile of v5, /device:TPU:1, one launch (start us, length us, event | category | flops | bytes accessed | tf_op | source)
XLA Modules:
  0.0 172.5 jit_solution(6818219393430903842)
XLA Ops:
  1.5 5.3 %fusion.6 = f32[64,16,256]{2,0,1:T(8,128)S(1)} fusion(f32[16,256,256]{2,1,0:T(8,128)} %param.9, f32[16,256]{1,0:T(8,128)S(1)} %fusion.12, f32[64,16,256]{2,1,0:T(8,128)} %param.7), kind=kOutput, calls=%fused_computation.7 | convolution fusion | flops 404750336 | bytes 6307840 | tf_op jit(solution)/shard_map/clt,lst->cls/dot_general | solution.py:115
  6.9 1.0 copy-done.2
  7.9 1.2 convolution_bitcast_fusion.1
  9.1 1.3 copy.19
  10.4 6.7 %shard_map.86 = f32[4096,64]{1,0:T(8,128)} custom-call(s32[2048]{0:T(1024)} %bitcast.80, f32[2048,64]{1,0:T(8,128)} %bitcast.78), custom_call_target="tpu_custom_call" | custom-call | tf_op jit(solution)/shard_map/pallas_call | solution.py:34
  17.1 1.9 %reshape_reshape.7 = f32[32,2,8,512]{3,2,1,0:T(8,128)S(1)} reshape(f32[4096,64]{1,0:T(8,128)} %shard_map.86) | data formatting | bytes 2097152 | tf_op jit(solution)/shard_map/reshape;reshape | solution.py:75
  19.1 3.3 %collective-permute-start.3 = (f32[32,8,512]{2,1,0:T(8,128)S(1)}, f32[32,8,512]{2,1,0:T(8,128)S(1)}, u32[]{:S(2)}, u32[]{:S(2)}) collective-permute-start(f32[32,8,512]{2,1,0:T(8,128)S(1)} %select_bitcast_fusion.1), channel_id=1, source_target_pairs={{0,4},{4,0},{1,5},{5,1},{2,6},{6,2},{3,7},{7,3},{8,12},{12,8},{9,1... | collective-permute-start | bytes 1572872 | tf_op jit(solution)/shard_map/ppermute | solution.py:78
  22.4 1.5 collective-permute-done.3
  24.9 9.5 %all-to-all-start = ((f32[32,8,512]{2,1,0:T(8,128)}), f32[32,8,512]{2,1,0:T(8,128)S(1)}, u32[]{:S(2)}, u32[]{:S(2)}) async-start(f32[32,8,512]{2,1,0:T(8,128)} %fusion.11), calls=%async_computation | async-start | bytes 1048576 | tf_op jit(solution)/shard_map/all_to_all | solution.py:79
  34.5 14.1 %all-to-all-done = f32[32,8,512]{2,1,0:T(8,128)S(1)} async-done(((f32[32,8,512]{2,1,0:T(8,128)}), f32[32,8,512]{2,1,0:T(8,128)S(1)}, u32[]{:S(2)}, u32[]{:S(2)}) %all-to-all-start) | async-done | bytes 524320 | tf_op jit(solution)/shard_map/all_to_all | solution.py:79
  48.8 1.1 broadcast_in_dim.7
  49.9 9.6 %all-to-all-start.1 = ((f32[64,8,512]{2,1,0:T(8,128)}), f32[64,8,512]{2,1,0:T(8,128)}, u32[]{:S(2)}, u32[]{:S(2)}) async-start(f32[64,8,512]{2,1,0:T(8,128)} %broadcast_in_dim.7), calls=%async_computation.1 | async-start | bytes 2097152 | tf_op jit(solution)/shard_map/all_to_all | solution.py:87
  59.6 2.6 %collective-permute-start = (f32[64,1024]{1,0:T(8,128)S(1)}, f32[64,1024]{1,0:T(8,128)S(1)}, u32[]{:S(2)}, u32[]{:S(2)}) collective-permute-start(f32[64,1024]{1,0:T(8,128)S(1)} %copy-done.4), channel_id=1, source_target_pairs={{0,3},{1,0},{2,1},{3,2},{4,7},{5,4},{6,5},{7,6},{8,11},{9,8},{10,9... | collective-permute-start | bytes 786440 | tf_op jit(solution)/shard_map/ppermute | solution.py:95
  64.0 4.1 %collective-permute-done = f32[64,1024]{1,0:T(8,128)S(1)} collective-permute-done((f32[64,1024]{1,0:T(8,128)S(1)}, f32[64,1024]{1,0:T(8,128)S(1)}, u32[]{:S(2)}, u32[]{:S(2)}) %collective-permute-start) | collective-permute-done | bytes 262176 | tf_op jit(solution)/shard_map/ppermute | solution.py:95
  68.8 2.1 %collective-permute-done.1 = f32[64,1024]{1,0:T(8,128)S(1)} collective-permute-done((f32[64,1024]{1,0:T(8,128)S(1)}, f32[64,1024]{1,0:T(8,128)S(1)}, u32[]{:S(2)}, u32[]{:S(2)}) %collective-permute-start.1) | collective-permute-done | bytes 262176 | tf_op jit(solution)/shard_map/ppermute | solution.py:95
  71.5 6.0 %collective-permute-done.2 = f32[64,1024]{1,0:T(8,128)S(1)} collective-permute-done((f32[64,1024]{1,0:T(8,128)S(1)}, f32[64,1024]{1,0:T(8,128)S(1)}, u32[]{:S(2)}, u32[]{:S(2)}) %collective-permute-start.2) | collective-permute-done | bytes 262176 | tf_op jit(solution)/shard_map/ppermute | solution.py:95
  81.2 1.3 dynamic-slice_bitcast_fusion
  82.6 5.4 %all-to-all-done.1 = f32[64,8,512]{2,1,0:T(8,128)} async-done(((f32[64,8,512]{2,1,0:T(8,128)}), f32[64,8,512]{2,1,0:T(8,128)}, u32[]{:S(2)}, u32[]{:S(2)}) %all-to-all-start.1) | async-done | bytes 1048608 | tf_op jit(solution)/shard_map/all_to_all | solution.py:87
  88.0 2.7 %reshape.77 = f32[4096,64]{1,0:T(8,128)} reshape(f32[64,8,512]{2,1,0:T(8,128)} %all-to-all-done.1) | data formatting | bytes 2097152 | tf_op jit(solution)/shard_map/reshape | solution.py:88
  90.7 2.4 %fusion.13 = f32[64,64]{1,0:T(8,128)S(1)} fusion(f32[64,4096]{1,0:T(8,128)S(1)} %bitcast.75, f32[4096,64]{1,0:T(8,128)} %reshape.77), kind=kOutput, calls=%fused_computation.33 | convolution fusion | flops 100663296 | bytes 2113536 | tf_op jit(solution)/shard_map/jc,ij->ic/dot_general | solution.py:130
  93.1 3.1 %fusion.14 = f32[4096,64]{1,0:T(8,128)} fusion(f32[64,4096]{1,0:T(8,128)S(1)} %bitcast.76, f32[64,64]{1,0:T(8,128)S(1)} %fusion.13), kind=kOutput, calls=%fused_computation.34 | convolution fusion | flops 100663296 | bytes 2113536 | tf_op jit(solution)/shard_map/ic,ij->jc/dot_general | solution.py:136
  96.2 1.9 %reshape_reshape.8 = f32[32,2,8,512]{3,2,1,0:T(8,128)S(1)} reshape(f32[4096,64]{1,0:T(8,128)} %fusion.14) | data formatting | bytes 2097152 | tf_op jit(solution)/shard_map/reshape;reshape | solution.py:75
  98.4 1.8 %collective-permute-done.4 = f32[32,8,512]{2,1,0:T(8,128)S(1)} collective-permute-done((f32[32,8,512]{2,1,0:T(8,128)S(1)}, f32[32,8,512]{2,1,0:T(8,128)S(1)}, u32[]{:S(2)}, u32[]{:S(2)}) %collective-permute-start.4) | collective-permute-done | bytes 524320 | tf_op jit(solution)/shard_map/ppermute | solution.py:78
  100.4 19.4 %all_to_all.20 = f32[32,8,512]{2,1,0:T(8,128)S(1)} all-to-all(f32[32,8,512]{2,1,0:T(8,128)S(1)} %bitcast_add_fusion), channel_id=1, replica_groups=mesh['y'=4,'z'=8,'core'=2,'rhs'=4] {'y','z'}, dimensions={0} | all-to-all | bytes 1048576 | tf_op jit(solution)/shard_map/all_to_all | solution.py:79
  119.8 1.1 broadcast_in_dim.8
  120.9 9.4 %all-to-all-start.3 = ((f32[64,8,512]{2,1,0:T(8,128)}), f32[64,8,512]{2,1,0:T(8,128)S(1)}, u32[]{:S(2)}, u32[]{:S(2)}) async-start(f32[64,8,512]{2,1,0:T(8,128)} %broadcast_in_dim.8), calls=%async_computation.3 | async-start | bytes 2097152 | tf_op jit(solution)/shard_map/all_to_all | solution.py:87
  131.1 27.7 %all-to-all-done.3 = f32[64,8,512]{2,1,0:T(8,128)S(1)} async-done(((f32[64,8,512]{2,1,0:T(8,128)}), f32[64,8,512]{2,1,0:T(8,128)S(1)}, u32[]{:S(2)}, u32[]{:S(2)}) %all-to-all-start.3) | async-done | bytes 1048608 | tf_op jit(solution)/shard_map/all_to_all | solution.py:87
  158.9 1.7 %reshape.78.table_ref = f32[4096,64]{1,0:T(8,128)} reshape(f32[64,8,512]{2,1,0:T(8,128)S(1)} %all-to-all-done.3) | data formatting | bytes 2097152 | tf_op jit(solution)/shard_map/reshape | solution.py:88
  160.6 5.7 %shard_map.87 = f32[2048,64]{1,0:T(8,128)} custom-call(s32[2048]{0:T(1024)} %bitcast.81, f32[4096,64]{1,0:T(8,128)} %reshape.78.table_ref), custom_call_target="tpu_custom_call" | custom-call | tf_op jit(solution)/shard_map/pallas_call | solution.py:60
  166.3 2.6 %fusion.8 = f32[64,16,256]{2,0,1:T(8,128)S(1)} fusion(f32[64,16,256]{2,0,1:T(8,128)S(1)} %copy-done.3, f32[16,128,64]{2,1,0:T(8,128)} %bitcast.77, f32[16,128,256]{2,1,0:T(8,128)S(1)} %copy-done), kind=kOutput, calls=%fused_computation.10 | convolution fusion | flops 201588736 | bytes 4718592 | tf_op jit(solution)/shard_map/nvr,nvb->rnb/dot_general | solution.py:140
  168.9 1.9 %fusion.7 = f32[64,16,256]{2,0,1:T(8,128)S(1)} fusion(f32[64,16,256]{2,0,1:T(8,128)S(1)} %fusion.8, f32[16,256,256]{2,1,0:T(8,128)S(1)} %copy-done.1, f32[16,256]{1,0:T(8,128)S(1)} %fusion.12), kind=kOutput, calls=%fused_computation.8 | convolution fusion | flops 404750336 | bytes 6307840 | tf_op jit(solution)/shard_map/cls,lst->clt/dot_general | solution.py:143
  170.9 1.6 copy.27
  (36 shorter events, 10.4 us)
Async XLA Ops:
  0.6 7.2 %copy-start = (f32[16,128,256]{2,1,0:T(8,128)S(1)}, f32[16,128,256]{2,1,0:T(8,128)}, u32[]{:S(2)}) copy-start(f32[16,128,256]{2,1,0:T(8,128)} %param.10) | copy-start | bytes 6291460
  6.9 1.0 copy-start.2
  19.0 15.4 %copy-start.5 = (f32[64,64]{1,0:T(8,128)S(1)}, f32[64,64]{1,0:T(8,128)}, u32[]{:S(2)}) copy-start(f32[64,64]{1,0:T(8,128)} %param.8) | copy-start | bytes 49156
  19.1 4.8 %collective-permute-start.3 = (f32[32,8,512]{2,1,0:T(8,128)S(1)}, f32[32,8,512]{2,1,0:T(8,128)S(1)}, u32[]{:S(2)}, u32[]{:S(2)}) collective-permute-start(f32[32,8,512]{2,1,0:T(8,128)S(1)} %select_bitcast_fusion.1), channel_id=1, source_target_pairs={{0,4},{4,0},{1,5},{5,1},{2,6},{6,2},{3,7},{7,3},{8,12},{12,8},{9,1... | collective-permute-start | bytes 1572872 | tf_op jit(solution)/shard_map/ppermute | solution.py:78
  24.9 23.7 %all-to-all-start = ((f32[32,8,512]{2,1,0:T(8,128)}), f32[32,8,512]{2,1,0:T(8,128)S(1)}, u32[]{:S(2)}, u32[]{:S(2)}) async-start(f32[32,8,512]{2,1,0:T(8,128)} %fusion.11), calls=%async_computation | async-start | bytes 1048576 | tf_op jit(solution)/shard_map/all_to_all | solution.py:79
  34.4 25.1 %copy-start.4 = (f32[64,1024]{1,0:T(8,128)S(1)}, f32[64,1024]{1,0:T(8,128)}, u32[]{:S(2)}) copy-start(f32[64,1024]{1,0:T(8,128)} %param.13) | copy-start | bytes 786436
  49.9 38.1 %all-to-all-start.1 = ((f32[64,8,512]{2,1,0:T(8,128)}), f32[64,8,512]{2,1,0:T(8,128)}, u32[]{:S(2)}, u32[]{:S(2)}) async-start(f32[64,8,512]{2,1,0:T(8,128)} %broadcast_in_dim.7), calls=%async_computation.1 | async-start | bytes 2097152 | tf_op jit(solution)/shard_map/all_to_all | solution.py:87
  59.6 8.5 %collective-permute-start = (f32[64,1024]{1,0:T(8,128)S(1)}, f32[64,1024]{1,0:T(8,128)S(1)}, u32[]{:S(2)}, u32[]{:S(2)}) collective-permute-start(f32[64,1024]{1,0:T(8,128)S(1)} %copy-done.4), channel_id=1, source_target_pairs={{0,3},{1,0},{2,1},{3,2},{4,7},{5,4},{6,5},{7,6},{8,11},{9,8},{10,9... | collective-permute-start | bytes 786440 | tf_op jit(solution)/shard_map/ppermute | solution.py:95
  62.1 8.7 %collective-permute-start.1 = (f32[64,1024]{1,0:T(8,128)S(1)}, f32[64,1024]{1,0:T(8,128)S(1)}, u32[]{:S(2)}, u32[]{:S(2)}) collective-permute-start(f32[64,1024]{1,0:T(8,128)S(1)} %copy-done.4), channel_id=1, source_target_pairs={{0,2},{1,3},{2,0},{3,1},{4,6},{5,7},{6,4},{7,5},{8,10},{9,11},{10,... | collective-permute-start | bytes 786440 | tf_op jit(solution)/shard_map/ppermute | solution.py:95
  62.6 14.9 %collective-permute-start.2 = (f32[64,1024]{1,0:T(8,128)S(1)}, f32[64,1024]{1,0:T(8,128)S(1)}, u32[]{:S(2)}, u32[]{:S(2)}) collective-permute-start(f32[64,1024]{1,0:T(8,128)S(1)} %copy-done.4), channel_id=1, source_target_pairs={{0,1},{1,2},{2,3},{3,0},{4,5},{5,6},{6,7},{7,4},{8,9},{9,10},{10,1... | collective-permute-start | bytes 786440 | tf_op jit(solution)/shard_map/ppermute | solution.py:95
  98.3 2.0 %collective-permute-start.4 = (f32[32,8,512]{2,1,0:T(8,128)S(1)}, f32[32,8,512]{2,1,0:T(8,128)S(1)}, u32[]{:S(2)}, u32[]{:S(2)}) collective-permute-start(f32[32,8,512]{2,1,0:T(8,128)S(1)} %select_bitcast_fusion), channel_id=1, source_target_pairs={{0,4},{4,0},{1,5},{5,1},{2,6},{6,2},{3,7},{7,3},{8,12},{12,8},{9,1... | collective-permute-start | bytes 1572872 | tf_op jit(solution)/shard_map/ppermute | solution.py:78
  120.9 37.9 %all-to-all-start.3 = ((f32[64,8,512]{2,1,0:T(8,128)}), f32[64,8,512]{2,1,0:T(8,128)S(1)}, u32[]{:S(2)}, u32[]{:S(2)}) async-start(f32[64,8,512]{2,1,0:T(8,128)} %broadcast_in_dim.8), calls=%async_computation.3 | async-start | bytes 2097152 | tf_op jit(solution)/shard_map/all_to_all | solution.py:87
  160.6 5.7 %copy-start.3 = (f32[64,16,256]{2,0,1:T(8,128)S(1)}, f32[64,16,256]{2,0,1:T(8,128)}, u32[]{:S(2)}) copy-start(f32[64,16,256]{2,0,1:T(8,128)} %copy-done.2) | copy-start | bytes 3145732
  166.3 2.6 %copy-start.1 = (f32[16,256,256]{2,1,0:T(8,128)S(1)}, f32[16,256,256]{2,1,0:T(8,128)}, u32[]{:S(2)}) copy-start(f32[16,256,256]{2,1,0:T(8,128)} %param.9) | copy-start | bytes 12582916

commit v6 on v5

--- a/solution.py
+++ b/solution.py
@@ -9,7 +9,7 @@
 LEAF_AXES = ("y", "z", "core")
 
 
-GROUP = 16
+GROUP = 32
 
 
 def scatter_rows(rows, updates, order):

time: 173 us -> 173 us (level)
  no operation moved by 1% of the time
where the time goes in v6:
time: 173 us
  waiting for transfers between devices  62.8 us (36%)
  starting transfers between devices  35.7 us (21%)
  local copies, waits for them, and re-layouts  22.6 us (13%)
  blocking collectives  19.4 us (11%)
  matrix products  16.6 us (10%)
  Pallas kernels  12.5 us (7%)
  other arithmetic  2.22 us (1%)
    all_to_all x2, waiting for transfers between devices, share_all(): gathered = lax.all_to_all(copies, LEAF_AXES, 0, 0, tiled=False)  33.1 us
    all_to_all x1, blocking collectives, owner_sum(): spread = lax.all_to_all(paired, ('y', 'z'), 0, 0, tiled=False)  19.4 us
    all_to_all x2, starting transfers between devices, share_all(): gathered = lax.all_to_all(copies, LEAF_AXES, 0, 0, tiled=False)  19 us
    all_to_all x1, waiting for transfers between devices, owner_sum(): spread = lax.all_to_all(paired, ('y', 'z'), 0, 0, tiled=False)  14.1 us
    ppermute x3, waiting for transfers between devices, gather_columns(): lax.ppermute(part, 'rhs', [(i, (i + step) % count) for i in range(count)])  12.2 us
    unnamed x23, local copies, waits for them, and re-layouts  9.7 us
    all_to_all x1, starting transfers between devices, owner_sum(): spread = lax.all_to_all(paired, ('y', 'z'), 0, 0, tiled=False)  9.49 us
    pallas_call x1, Pallas kernels, scatter_rows(): pl.pallas_call(kernel, out_shape=jax.ShapeDtypeStruct((order, columns), j...  7.11 us
  transfers between devices with their start and end apart: 8, of which 8 were waited for; matrix products, arithmetic and copies ran while one was open for 5% of the time, Pallas kernels for 0%

profile of v6, /device:TPU:1, one launch (start us, length us, event | category | flops | bytes accessed | tf_op | source)
XLA Modules:
  0.0 172.6 jit_solution(13812058465411812544)
XLA Ops:
  1.5 5.3 %fusion.6 = f32[64,16,256]{2,0,1:T(8,128)S(1)} fusion(f32[16,256,256]{2,1,0:T(8,128)} %param.9, f32[16,256]{1,0:T(8,128)S(1)} %fusion.12, f32[64,16,256]{2,1,0:T(8,128)} %param.7), kind=kOutput, calls=%fused_computation.7 | convolution fusion | flops 404750336 | bytes 6307840 | tf_op jit(solution)/shard_map/clt,lst->cls/dot_general | solution.py:115
  6.9 1.0 copy-done.2
  7.9 1.2 convolution_bitcast_fusion.1
  9.1 1.3 copy.19
  10.4 7.1 %shard_map.86 = f32[4096,64]{1,0:T(8,128)} custom-call(s32[2048]{0:T(1024)} %bitcast.80, f32[2048,64]{1,0:T(8,128)} %bitcast.78), custom_call_target="tpu_custom_call" | custom-call | tf_op jit(solution)/shard_map/pallas_call | solution.py:34
  17.5 1.9 %reshape_reshape.7 = f32[32,2,8,512]{3,2,1,0:T(8,128)S(1)} reshape(f32[4096,64]{1,0:T(8,128)} %shard_map.86) | data formatting | bytes 2097152 | tf_op jit(solution)/shard_map/reshape;reshape | solution.py:75
  19.5 3.3 %collective-permute-start.3 = (f32[32,8,512]{2,1,0:T(8,128)S(1)}, f32[32,8,512]{2,1,0:T(8,128)S(1)}, u32[]{:S(2)}, u32[]{:S(2)}) collective-permute-start(f32[32,8,512]{2,1,0:T(8,128)S(1)} %select_bitcast_fusion.1), channel_id=1, source_target_pairs={{0,4},{4,0},{1,5},{5,1},{2,6},{6,2},{3,7},{7,3},{8,12},{12,8},{9,1... | collective-permute-start | bytes 1572872 | tf_op jit(solution)/shard_map/ppermute | solution.py:78
  22.8 1.5 collective-permute-done.3
  25.3 9.5 %all-to-all-start = ((f32[32,8,512]{2,1,0:T(8,128)}), f32[32,8,512]{2,1,0:T(8,128)S(1)}, u32[]{:S(2)}, u32[]{:S(2)}) async-start(f32[32,8,512]{2,1,0:T(8,128)} %fusion.11), calls=%async_computation | async-start | bytes 1048576 | tf_op jit(solution)/shard_map/all_to_all | solution.py:79
  34.9 14.1 %all-to-all-done = f32[32,8,512]{2,1,0:T(8,128)S(1)} async-done(((f32[32,8,512]{2,1,0:T(8,128)}), f32[32,8,512]{2,1,0:T(8,128)S(1)}, u32[]{:S(2)}, u32[]{:S(2)}) %all-to-all-start) | async-done | bytes 524320 | tf_op jit(solution)/shard_map/all_to_all | solution.py:79
  49.2 1.1 broadcast_in_dim.7
  50.3 9.6 %all-to-all-start.1 = ((f32[64,8,512]{2,1,0:T(8,128)}), f32[64,8,512]{2,1,0:T(8,128)}, u32[]{:S(2)}, u32[]{:S(2)}) async-start(f32[64,8,512]{2,1,0:T(8,128)} %broadcast_in_dim.7), calls=%async_computation.1 | async-start | bytes 2097152 | tf_op jit(solution)/shard_map/all_to_all | solution.py:87
  60.0 2.6 %collective-permute-start = (f32[64,1024]{1,0:T(8,128)S(1)}, f32[64,1024]{1,0:T(8,128)S(1)}, u32[]{:S(2)}, u32[]{:S(2)}) collective-permute-start(f32[64,1024]{1,0:T(8,128)S(1)} %copy-done.4), channel_id=1, source_target_pairs={{0,3},{1,0},{2,1},{3,2},{4,7},{5,4},{6,5},{7,6},{8,11},{9,8},{10,9... | collective-permute-start | bytes 786440 | tf_op jit(solution)/shard_map/ppermute | solution.py:95
  64.4 4.1 %collective-permute-done = f32[64,1024]{1,0:T(8,128)S(1)} collective-permute-done((f32[64,1024]{1,0:T(8,128)S(1)}, f32[64,1024]{1,0:T(8,128)S(1)}, u32[]{:S(2)}, u32[]{:S(2)}) %collective-permute-start) | collective-permute-done | bytes 262176 | tf_op jit(solution)/shard_map/ppermute | solution.py:95
  69.2 2.1 %collective-permute-done.1 = f32[64,1024]{1,0:T(8,128)S(1)} collective-permute-done((f32[64,1024]{1,0:T(8,128)S(1)}, f32[64,1024]{1,0:T(8,128)S(1)}, u32[]{:S(2)}, u32[]{:S(2)}) %collective-permute-start.1) | collective-permute-done | bytes 262176 | tf_op jit(solution)/shard_map/ppermute | solution.py:95
  72.0 6.0 %collective-permute-done.2 = f32[64,1024]{1,0:T(8,128)S(1)} collective-permute-done((f32[64,1024]{1,0:T(8,128)S(1)}, f32[64,1024]{1,0:T(8,128)S(1)}, u32[]{:S(2)}, u32[]{:S(2)}) %collective-permute-start.2) | collective-permute-done | bytes 262176 | tf_op jit(solution)/shard_map/ppermute | solution.py:95
  81.6 1.3 dynamic-slice_bitcast_fusion
  83.0 5.4 %all-to-all-done.1 = f32[64,8,512]{2,1,0:T(8,128)} async-done(((f32[64,8,512]{2,1,0:T(8,128)}), f32[64,8,512]{2,1,0:T(8,128)}, u32[]{:S(2)}, u32[]{:S(2)}) %all-to-all-start.1) | async-done | bytes 1048608 | tf_op jit(solution)/shard_map/all_to_all | solution.py:87
  88.4 2.7 %reshape.77 = f32[4096,64]{1,0:T(8,128)} reshape(f32[64,8,512]{2,1,0:T(8,128)} %all-to-all-done.1) | data formatting | bytes 2097152 | tf_op jit(solution)/shard_map/reshape | solution.py:88
  91.1 2.4 %fusion.13 = f32[64,64]{1,0:T(8,128)S(1)} fusion(f32[64,4096]{1,0:T(8,128)S(1)} %bitcast.75, f32[4096,64]{1,0:T(8,128)} %reshape.77), kind=kOutput, calls=%fused_computation.33 | convolution fusion | flops 100663296 | bytes 2113536 | tf_op jit(solution)/shard_map/jc,ij->ic/dot_general | solution.py:130
  93.5 3.1 %fusion.14 = f32[4096,64]{1,0:T(8,128)} fusion(f32[64,4096]{1,0:T(8,128)S(1)} %bitcast.76, f32[64,64]{1,0:T(8,128)S(1)} %fusion.13), kind=kOutput, calls=%fused_computation.34 | convolution fusion | flops 100663296 | bytes 2113536 | tf_op jit(solution)/shard_map/ic,ij->jc/dot_general | solution.py:136
  96.6 1.9 %reshape_reshape.8 = f32[32,2,8,512]{3,2,1,0:T(8,128)S(1)} reshape(f32[4096,64]{1,0:T(8,128)} %fusion.14) | data formatting | bytes 2097152 | tf_op jit(solution)/shard_map/reshape;reshape | solution.py:75
  98.8 1.8 %collective-permute-done.4 = f32[32,8,512]{2,1,0:T(8,128)S(1)} collective-permute-done((f32[32,8,512]{2,1,0:T(8,128)S(1)}, f32[32,8,512]{2,1,0:T(8,128)S(1)}, u32[]{:S(2)}, u32[]{:S(2)}) %collective-permute-start.4) | collective-permute-done | bytes 524320 | tf_op jit(solution)/shard_map/ppermute | solution.py:78
  100.8 19.4 %all_to_all.20 = f32[32,8,512]{2,1,0:T(8,128)S(1)} all-to-all(f32[32,8,512]{2,1,0:T(8,128)S(1)} %bitcast_add_fusion), channel_id=1, replica_groups=mesh['y'=4,'z'=8,'core'=2,'rhs'=4] {'y','z'}, dimensions={0} | all-to-all | bytes 1048576 | tf_op jit(solution)/shard_map/all_to_all | solution.py:79
  120.2 1.1 broadcast_in_dim.8
  121.3 9.4 %all-to-all-start.3 = ((f32[64,8,512]{2,1,0:T(8,128)}), f32[64,8,512]{2,1,0:T(8,128)S(1)}, u32[]{:S(2)}, u32[]{:S(2)}) async-start(f32[64,8,512]{2,1,0:T(8,128)} %broadcast_in_dim.8), calls=%async_computation.3 | async-start | bytes 2097152 | tf_op jit(solution)/shard_map/all_to_all | solution.py:87
  131.5 27.7 %all-to-all-done.3 = f32[64,8,512]{2,1,0:T(8,128)S(1)} async-done(((f32[64,8,512]{2,1,0:T(8,128)}), f32[64,8,512]{2,1,0:T(8,128)S(1)}, u32[]{:S(2)}, u32[]{:S(2)}) %all-to-all-start.3) | async-done | bytes 1048608 | tf_op jit(solution)/shard_map/all_to_all | solution.py:87
  159.3 1.7 %reshape.78.table_ref = f32[4096,64]{1,0:T(8,128)} reshape(f32[64,8,512]{2,1,0:T(8,128)S(1)} %all-to-all-done.3) | data formatting | bytes 2097152 | tf_op jit(solution)/shard_map/reshape | solution.py:88
  161.0 5.4 %shard_map.87 = f32[2048,64]{1,0:T(8,128)} custom-call(s32[2048]{0:T(1024)} %bitcast.81, f32[4096,64]{1,0:T(8,128)} %reshape.78.table_ref), custom_call_target="tpu_custom_call" | custom-call | tf_op jit(solution)/shard_map/pallas_call | solution.py:60
  166.4 2.6 %fusion.8 = f32[64,16,256]{2,0,1:T(8,128)S(1)} fusion(f32[64,16,256]{2,0,1:T(8,128)S(1)} %copy-done.3, f32[16,128,64]{2,1,0:T(8,128)} %bitcast.77, f32[16,128,256]{2,1,0:T(8,128)S(1)} %copy-done), kind=kOutput, calls=%fused_computation.10 | convolution fusion | flops 201588736 | bytes 4718592 | tf_op jit(solution)/shard_map/nvr,nvb->rnb/dot_general | solution.py:140
  169.0 1.9 %fusion.7 = f32[64,16,256]{2,0,1:T(8,128)S(1)} fusion(f32[64,16,256]{2,0,1:T(8,128)S(1)} %fusion.8, f32[16,256,256]{2,1,0:T(8,128)S(1)} %copy-done.1, f32[16,256]{1,0:T(8,128)S(1)} %fusion.12), kind=kOutput, calls=%fused_computation.8 | convolution fusion | flops 404750336 | bytes 6307840 | tf_op jit(solution)/shard_map/cls,lst->clt/dot_general | solution.py:143
  171.0 1.6 copy.27
  (36 shorter events, 10.4 us)
Async XLA Ops:
  0.6 7.2 %copy-start = (f32[16,128,256]{2,1,0:T(8,128)S(1)}, f32[16,128,256]{2,1,0:T(8,128)}, u32[]{:S(2)}) copy-start(f32[16,128,256]{2,1,0:T(8,128)} %param.10) | copy-start | bytes 6291460
  6.9 1.0 copy-start.2
  19.4 15.4 %copy-start.5 = (f32[64,64]{1,0:T(8,128)S(1)}, f32[64,64]{1,0:T(8,128)}, u32[]{:S(2)}) copy-start(f32[64,64]{1,0:T(8,128)} %param.8) | copy-start | bytes 49156
  19.5 4.8 %collective-permute-start.3 = (f32[32,8,512]{2,1,0:T(8,128)S(1)}, f32[32,8,512]{2,1,0:T(8,128)S(1)}, u32[]{:S(2)}, u32[]{:S(2)}) collective-permute-start(f32[32,8,512]{2,1,0:T(8,128)S(1)} %select_bitcast_fusion.1), channel_id=1, source_target_pairs={{0,4},{4,0},{1,5},{5,1},{2,6},{6,2},{3,7},{7,3},{8,12},{12,8},{9,1... | collective-permute-start | bytes 1572872 | tf_op jit(solution)/shard_map/ppermute | solution.py:78
  25.3 23.7 %all-to-all-start = ((f32[32,8,512]{2,1,0:T(8,128)}), f32[32,8,512]{2,1,0:T(8,128)S(1)}, u32[]{:S(2)}, u32[]{:S(2)}) async-start(f32[32,8,512]{2,1,0:T(8,128)} %fusion.11), calls=%async_computation | async-start | bytes 1048576 | tf_op jit(solution)/shard_map/all_to_all | solution.py:79
  34.8 25.1 %copy-start.4 = (f32[64,1024]{1,0:T(8,128)S(1)}, f32[64,1024]{1,0:T(8,128)}, u32[]{:S(2)}) copy-start(f32[64,1024]{1,0:T(8,128)} %param.13) | copy-start | bytes 786436
  50.3 38.1 %all-to-all-start.1 = ((f32[64,8,512]{2,1,0:T(8,128)}), f32[64,8,512]{2,1,0:T(8,128)}, u32[]{:S(2)}, u32[]{:S(2)}) async-start(f32[64,8,512]{2,1,0:T(8,128)} %broadcast_in_dim.7), calls=%async_computation.1 | async-start | bytes 2097152 | tf_op jit(solution)/shard_map/all_to_all | solution.py:87
  60.0 8.5 %collective-permute-start = (f32[64,1024]{1,0:T(8,128)S(1)}, f32[64,1024]{1,0:T(8,128)S(1)}, u32[]{:S(2)}, u32[]{:S(2)}) collective-permute-start(f32[64,1024]{1,0:T(8,128)S(1)} %copy-done.4), channel_id=1, source_target_pairs={{0,3},{1,0},{2,1},{3,2},{4,7},{5,4},{6,5},{7,6},{8,11},{9,8},{10,9... | collective-permute-start | bytes 786440 | tf_op jit(solution)/shard_map/ppermute | solution.py:95
  62.5 8.7 %collective-permute-start.1 = (f32[64,1024]{1,0:T(8,128)S(1)}, f32[64,1024]{1,0:T(8,128)S(1)}, u32[]{:S(2)}, u32[]{:S(2)}) collective-permute-start(f32[64,1024]{1,0:T(8,128)S(1)} %copy-done.4), channel_id=1, source_target_pairs={{0,2},{1,3},{2,0},{3,1},{4,6},{5,7},{6,4},{7,5},{8,10},{9,11},{10,... | collective-permute-start | bytes 786440 | tf_op jit(solution)/shard_map/ppermute | solution.py:95
  63.0 14.9 %collective-permute-start.2 = (f32[64,1024]{1,0:T(8,128)S(1)}, f32[64,1024]{1,0:T(8,128)S(1)}, u32[]{:S(2)}, u32[]{:S(2)}) collective-permute-start(f32[64,1024]{1,0:T(8,128)S(1)} %copy-done.4), channel_id=1, source_target_pairs={{0,1},{1,2},{2,3},{3,0},{4,5},{5,6},{6,7},{7,4},{8,9},{9,10},{10,1... | collective-permute-start | bytes 786440 | tf_op jit(solution)/shard_map/ppermute | solution.py:95
  98.7 2.0 %collective-permute-start.4 = (f32[32,8,512]{2,1,0:T(8,128)S(1)}, f32[32,8,512]{2,1,0:T(8,128)S(1)}, u32[]{:S(2)}, u32[]{:S(2)}) collective-permute-start(f32[32,8,512]{2,1,0:T(8,128)S(1)} %select_bitcast_fusion), channel_id=1, source_target_pairs={{0,4},{4,0},{1,5},{5,1},{2,6},{6,2},{3,7},{7,3},{8,12},{12,8},{9,1... | collective-permute-start | bytes 1572872 | tf_op jit(solution)/shard_map/ppermute | solution.py:78
  121.3 37.9 %all-to-all-start.3 = ((f32[64,8,512]{2,1,0:T(8,128)}), f32[64,8,512]{2,1,0:T(8,128)S(1)}, u32[]{:S(2)}, u32[]{:S(2)}) async-start(f32[64,8,512]{2,1,0:T(8,128)} %broadcast_in_dim.8), calls=%async_computation.3 | async-start | bytes 2097152 | tf_op jit(solution)/shard_map/all_to_all | solution.py:87
  161.0 5.4 %copy-start.3 = (f32[64,16,256]{2,0,1:T(8,128)S(1)}, f32[64,16,256]{2,0,1:T(8,128)}, u32[]{:S(2)}) copy-start(f32[64,16,256]{2,0,1:T(8,128)} %copy-done.2) | copy-start | bytes 3145732
  166.4 2.6 %copy-start.1 = (f32[16,256,256]{2,1,0:T(8,128)S(1)}, f32[16,256,256]{2,1,0:T(8,128)}, u32[]{:S(2)}) copy-start(f32[16,256,256]{2,1,0:T(8,128)} %param.9) | copy-start | bytes 12582916

commit v7 on v6

--- a/solution.py
+++ b/solution.py
@@ -112,7 +112,16 @@
     slot_index = lax.broadcasted_iota(jnp.int32, (leaf_count, leaf_width), 1)
     live_mask = (slot_index < leaf_sizes[:, None]).astype(jnp.float32)
     masked = leaf_inverse * live_mask[:, :, None] * live_mask[:, None, :]
-    leaf_forward_sweep = jnp.einsum("clt,lst->cls", leaf_rhs, masked, precision=largest_entry)
+    half = leaf_width // 2
+    leaf_forward_sweep = jnp.concatenate(
+        [
+            jnp.einsum(
+                "clt,lst->cls", leaf_rhs[:, :, :half], masked[:, :half, :half], precision=largest_entry
+            ),
+            jnp.einsum("clt,lst->cls", leaf_rhs, masked[:, half:, :], precision=largest_entry),
+        ],
+        axis=2,
+    )
     update_terms = jnp.einsum(
         "dwu,wqu->wqd", leaf_forward_sweep, leaf_offdiagonal_block, precision=largest_entry
     )
@@ -140,7 +149,18 @@
     adjusted_values = leaf_forward_sweep - jnp.einsum(
         "nvr,nvb->rnb", selected_rows, leaf_offdiagonal_block, precision=largest_entry
     )
-    leaf_solution = jnp.einsum("cls,lst->clt", adjusted_values, masked, precision=largest_entry)
+    leaf_solution = jnp.concatenate(
+        [
+            jnp.einsum("cls,lst->clt", adjusted_values, masked[:, :, :half], precision=largest_entry),
+            jnp.einsum(
+                "cls,lst->clt",
+                adjusted_values[:, :, half:],
+                masked[:, half:, half:],
+                precision=largest_entry,
+            ),
+        ],
+        axis=2,
+    )
     return (leaf_solution, root_solution.T)
 
 

time: 173 us -> 175 us (1.012)
  matrix products: 16.6 us -> 13.5 us
  other arithmetic: 2.22 us -> 4.99 us
  local copies, waits for them, and re-layouts: 22.6 us -> 24.4 us
    dot_general x2 -> x4, matrix products: 7.27 us -> 4.15 us  [the longest x1 1.62 us: on_device(): jnp.einsum('clt,lst->cls', leaf_rhs, masked[:, half:, :], precision=large...]
    mul x0 -> x1, other arithmetic: none -> 2.67 us  [on_device(): masked = leaf_inverse * live_mask[:, :, None] * live_mask[:, None, :]]
    unnamed x23 -> x32, local copies, waits for them, and re-layouts: 9.7 us -> 11.5 us
where the time goes in v7:
time: 175 us; the launch traced here: 174 us
  waiting for transfers between devices  62.7 us (36%)
  starting transfers between devices  35.7 us (20%)
  local copies, waits for them, and re-layouts  24.4 us (14%)
  blocking collectives  19.4 us (11%)
  matrix products  13.5 us (8%)
  Pallas kernels  12.5 us (7%)
  other arithmetic  4.99 us (3%)
    all_to_all x2, waiting for transfers between devices, share_all(): gathered = lax.all_to_all(copies, LEAF_AXES, 0, 0, tiled=False)  33.1 us
    all_to_all x1, blocking collectives, owner_sum(): spread = lax.all_to_all(paired, ('y', 'z'), 0, 0, tiled=False)  19.4 us
    all_to_all x2, starting transfers between devices, share_all(): gathered = lax.all_to_all(copies, LEAF_AXES, 0, 0, tiled=False)  19 us
    all_to_all x1, waiting for transfers between devices, owner_sum(): spread = lax.all_to_all(paired, ('y', 'z'), 0, 0, tiled=False)  14.1 us
    ppermute x3, waiting for transfers between devices, gather_columns(): lax.ppermute(part, 'rhs', [(i, (i + step) % count) for i in range(count)])  12.1 us
    unnamed x32, local copies, waits for them, and re-layouts  11.5 us
    all_to_all x1, starting transfers between devices, owner_sum(): spread = lax.all_to_all(paired, ('y', 'z'), 0, 0, tiled=False)  9.5 us
    pallas_call x1, Pallas kernels, scatter_rows(): pl.pallas_call(kernel, out_shape=jax.ShapeDtypeStruct((order, columns), j...  7.12 us
  transfers between devices with their start and end apart: 8, of which 8 were waited for; matrix products, arithmetic and copies ran while one was open for 5% of the time, Pallas kernels for 0%

profile of v7, /device:TPU:1, one launch (start us, length us, event | category | flops | bytes accessed | tf_op | source)
XLA Modules:
  0.0 174.0 jit_solution(1133251339738641570)
XLA Ops:
  1.5 1.8 %copy.18 = f32[64,16,256]{2,0,1:T(8,128)S(1)} copy(f32[64,16,256]{2,1,0:T(8,128)} %param.7) | data formatting | bytes 2097152 | tf_op args[0]
  3.4 2.7 %multiply_multiply_fusion = f32[16,256,256]{2,1,0:T(8,128)S(1)} fusion(f32[16,256,256]{2,1,0:T(8,128)} %param.9, f32[16,256]{1,0:T(8,128)S(1)} %fusion.17), kind=kLoop, calls=%fused_computation | loop fusion | flops 2097152 | bytes 8404992 | tf_op jit(solution)/shard_map/mul | solution.py:114
  6.1 1.6 fusion.8
  7.7 1.1 convolution_bitcast_fusion.3
  9.7 1.2 convolution_bitcast_fusion.2
  10.9 1.3 copy.22
  12.3 7.1 %shard_map.86 = f32[4096,64]{1,0:T(8,128)} custom-call(s32[2048]{0:T(1024)} %bitcast.83, f32[2048,64]{1,0:T(8,128)} %bitcast.81), custom_call_target="tpu_custom_call" | custom-call | tf_op jit(solution)/shard_map/pallas_call | solution.py:34
  19.4 1.9 %reshape_reshape.7 = f32[32,2,8,512]{3,2,1,0:T(8,128)S(1)} reshape(f32[4096,64]{1,0:T(8,128)} %shard_map.86) | data formatting | bytes 2097152 | tf_op jit(solution)/shard_map/reshape;reshape | solution.py:75
  21.4 3.3 %collective-permute-start.3 = (f32[32,8,512]{2,1,0:T(8,128)S(1)}, f32[32,8,512]{2,1,0:T(8,128)S(1)}, u32[]{:S(2)}, u32[]{:S(2)}) collective-permute-start(f32[32,8,512]{2,1,0:T(8,128)S(1)} %select_bitcast_fusion.1), channel_id=1, source_target_pairs={{0,4},{4,0},{1,5},{5,1},{2,6},{6,2},{3,7},{7,3},{8,12},{12,8},{9,1... | collective-permute-start | bytes 1572872 | tf_op jit(solution)/shard_map/ppermute | solution.py:78
  24.7 1.5 collective-permute-done.3
  27.2 9.5 %all-to-all-start = ((f32[32,8,512]{2,1,0:T(8,128)}), f32[32,8,512]{2,1,0:T(8,128)S(1)}, u32[]{:S(2)}, u32[]{:S(2)}) async-start(f32[32,8,512]{2,1,0:T(8,128)} %fusion.16), calls=%async_computation | async-start | bytes 1048576 | tf_op jit(solution)/shard_map/all_to_all | solution.py:79
  36.8 14.1 %all-to-all-done = f32[32,8,512]{2,1,0:T(8,128)S(1)} async-done(((f32[32,8,512]{2,1,0:T(8,128)}), f32[32,8,512]{2,1,0:T(8,128)S(1)}, u32[]{:S(2)}, u32[]{:S(2)}) %all-to-all-start) | async-done | bytes 524320 | tf_op jit(solution)/shard_map/all_to_all | solution.py:79
  51.1 1.1 broadcast_in_dim.7
  52.2 9.6 %all-to-all-start.1 = ((f32[64,8,512]{2,1,0:T(8,128)}), f32[64,8,512]{2,1,0:T(8,128)}, u32[]{:S(2)}, u32[]{:S(2)}) async-start(f32[64,8,512]{2,1,0:T(8,128)} %broadcast_in_dim.7), calls=%async_computation.1 | async-start | bytes 2097152 | tf_op jit(solution)/shard_map/all_to_all | solution.py:87
  61.8 2.6 %collective-permute-start = (f32[64,1024]{1,0:T(8,128)S(1)}, f32[64,1024]{1,0:T(8,128)S(1)}, u32[]{:S(2)}, u32[]{:S(2)}) collective-permute-start(f32[64,1024]{1,0:T(8,128)S(1)} %copy-done.8), channel_id=1, source_target_pairs={{0,3},{1,0},{2,1},{3,2},{4,7},{5,4},{6,5},{7,6},{8,11},{9,8},{10,9... | collective-permute-start | bytes 786440 | tf_op jit(solution)/shard_map/ppermute | solution.py:95
  66.2 4.1 %collective-permute-done = f32[64,1024]{1,0:T(8,128)S(1)} collective-permute-done((f32[64,1024]{1,0:T(8,128)S(1)}, f32[64,1024]{1,0:T(8,128)S(1)}, u32[]{:S(2)}, u32[]{:S(2)}) %collective-permute-start) | collective-permute-done | bytes 262176 | tf_op jit(solution)/shard_map/ppermute | solution.py:95
  71.0 2.1 %collective-permute-done.1 = f32[64,1024]{1,0:T(8,128)S(1)} collective-permute-done((f32[64,1024]{1,0:T(8,128)S(1)}, f32[64,1024]{1,0:T(8,128)S(1)}, u32[]{:S(2)}, u32[]{:S(2)}) %collective-permute-start.1) | collective-permute-done | bytes 262176 | tf_op jit(solution)/shard_map/ppermute | solution.py:95
  73.8 6.0 %collective-permute-done.2 = f32[64,1024]{1,0:T(8,128)S(1)} collective-permute-done((f32[64,1024]{1,0:T(8,128)S(1)}, f32[64,1024]{1,0:T(8,128)S(1)}, u32[]{:S(2)}, u32[]{:S(2)}) %collective-permute-start.2) | collective-permute-done | bytes 262176 | tf_op jit(solution)/shard_map/ppermute | solution.py:95
  83.5 1.3 dynamic-slice_bitcast_fusion
  84.9 5.4 %all-to-all-done.1 = f32[64,8,512]{2,1,0:T(8,128)} async-done(((f32[64,8,512]{2,1,0:T(8,128)}), f32[64,8,512]{2,1,0:T(8,128)}, u32[]{:S(2)}, u32[]{:S(2)}) %all-to-all-start.1) | async-done | bytes 1048608 | tf_op jit(solution)/shard_map/all_to_all | solution.py:87
  90.2 2.7 %reshape.77 = f32[4096,64]{1,0:T(8,128)} reshape(f32[64,8,512]{2,1,0:T(8,128)} %all-to-all-done.1) | data formatting | bytes 2097152 | tf_op jit(solution)/shard_map/reshape | solution.py:88
  93.0 2.4 %fusion.20 = f32[64,64]{1,0:T(8,128)S(1)} fusion(f32[64,4096]{1,0:T(8,128)S(1)} %bitcast.78, f32[4096,64]{1,0:T(8,128)} %reshape.77), kind=kOutput, calls=%fused_computation.40 | convolution fusion | flops 100663296 | bytes 2113536 | tf_op jit(solution)/shard_map/jc,ij->ic/dot_general | solution.py:139
  95.4 3.2 %fusion.21 = f32[4096,64]{1,0:T(8,128)} fusion(f32[64,4096]{1,0:T(8,128)S(1)} %bitcast.79, f32[64,64]{1,0:T(8,128)S(1)} %fusion.20), kind=kOutput, calls=%fused_computation.41 | convolution fusion | flops 100663296 | bytes 2113536 | tf_op jit(solution)/shard_map/ic,ij->jc/dot_general | solution.py:145
  98.5 1.9 %reshape_reshape.8 = f32[32,2,8,512]{3,2,1,0:T(8,128)S(1)} reshape(f32[4096,64]{1,0:T(8,128)} %fusion.21) | data formatting | bytes 2097152 | tf_op jit(solution)/shard_map/reshape;reshape | solution.py:75
  100.7 1.8 %collective-permute-done.4 = f32[32,8,512]{2,1,0:T(8,128)S(1)} collective-permute-done((f32[32,8,512]{2,1,0:T(8,128)S(1)}, f32[32,8,512]{2,1,0:T(8,128)S(1)}, u32[]{:S(2)}, u32[]{:S(2)}) %collective-permute-start.4) | collective-permute-done | bytes 524320 | tf_op jit(solution)/shard_map/ppermute | solution.py:78
  102.7 19.4 %all_to_all.20 = f32[32,8,512]{2,1,0:T(8,128)S(1)} all-to-all(f32[32,8,512]{2,1,0:T(8,128)S(1)} %bitcast_add_fusion), channel_id=1, replica_groups=mesh['y'=4,'z'=8,'core'=2,'rhs'=4] {'y','z'}, dimensions={0} | all-to-all | bytes 1048576 | tf_op jit(solution)/shard_map/all_to_all | solution.py:79
  123.2 9.4 %all-to-all-start.3 = ((f32[64,8,512]{2,1,0:T(8,128)}), f32[64,8,512]{2,1,0:T(8,128)S(1)}, u32[]{:S(2)}, u32[]{:S(2)}) async-start(f32[64,8,512]{2,1,0:T(8,128)} %broadcast_in_dim.8), calls=%async_computation.3 | async-start | bytes 2097152 | tf_op jit(solution)/shard_map/all_to_all | solution.py:87
  133.4 27.7 %all-to-all-done.3 = f32[64,8,512]{2,1,0:T(8,128)S(1)} async-done(((f32[64,8,512]{2,1,0:T(8,128)}), f32[64,8,512]{2,1,0:T(8,128)S(1)}, u32[]{:S(2)}, u32[]{:S(2)}) %all-to-all-start.3) | async-done | bytes 1048608 | tf_op jit(solution)/shard_map/all_to_all | solution.py:87
  161.2 1.8 %reshape.78.table_ref = f32[4096,64]{1,0:T(8,128)} reshape(f32[64,8,512]{2,1,0:T(8,128)S(1)} %all-to-all-done.3) | data formatting | bytes 2097152 | tf_op jit(solution)/shard_map/reshape | solution.py:88
  162.9 5.4 %shard_map.87 = f32[2048,64]{1,0:T(8,128)} custom-call(s32[2048]{0:T(1024)} %bitcast.84, f32[4096,64]{1,0:T(8,128)} %reshape.78.table_ref), custom_call_target="tpu_custom_call" | custom-call | tf_op jit(solution)/shard_map/pallas_call | solution.py:60
  168.3 2.6 %fusion.4 = f32[64,16,256]{2,0,1:T(8,128)S(1)} fusion(f32[16,128,64]{2,1,0:T(8,128)} %bitcast.80, f32[16,128,256]{2,1,0:T(8,128)S(1)} %copy-done, f32[64,16,128]{2,0,1:T(8,128)S(1)} %copy-done.4, f32[64,16,128]{2,0,1:T(8,128)S(1)} %copy-done.6), kind=kOutput, calls=%fused_computation.6 | convolution fusion | flops 201850880 | bytes 4718592 | tf_op jit(solution)/shard_map/nvr,nvb->rnb/dot_general | solution.py:149
  172.4 1.6 copy.31
  (49 shorter events, 13.9 us)
Async XLA Ops:
  0.6 9.1 %copy-start = (f32[16,128,256]{2,1,0:T(8,128)S(1)}, f32[16,128,256]{2,1,0:T(8,128)}, u32[]{:S(2)}) copy-start(f32[16,128,256]{2,1,0:T(8,128)} %param.10) | copy-start | bytes 6291460
  3.4 2.7 %copy-start.7 = (f32[64,16,256]{2,1,0:T(8,128)S(1)}, f32[64,16,256]{2,1,0:T(8,128)}, u32[]{:S(2)}) copy-start(f32[64,16,256]{2,1,0:T(8,128)} %param.7) | copy-start | bytes 3145732
  6.1 2.8 %copy-start.1 = (f32[16,256,256]{2,1,0:T(8,128)}, f32[16,256,256]{2,1,0:T(8,128)S(1)}, u32[]{:S(2)}) copy-start(f32[16,256,256]{2,1,0:T(8,128)S(1)} %multiply_multiply_fusion) | copy-start | bytes 12582916
  7.7 1.2 copy-start.3
  8.9 0.8 copy-start.5
  21.3 15.4 %copy-start.9 = (f32[64,64]{1,0:T(8,128)S(1)}, f32[64,64]{1,0:T(8,128)}, u32[]{:S(2)}) copy-start(f32[64,64]{1,0:T(8,128)} %param.8) | copy-start | bytes 49156
  21.4 4.8 %collective-permute-start.3 = (f32[32,8,512]{2,1,0:T(8,128)S(1)}, f32[32,8,512]{2,1,0:T(8,128)S(1)}, u32[]{:S(2)}, u32[]{:S(2)}) collective-permute-start(f32[32,8,512]{2,1,0:T(8,128)S(1)} %select_bitcast_fusion.1), channel_id=1, source_target_pairs={{0,4},{4,0},{1,5},{5,1},{2,6},{6,2},{3,7},{7,3},{8,12},{12,8},{9,1... | collective-permute-start | bytes 1572872 | tf_op jit(solution)/shard_map/ppermute | solution.py:78
  27.2 23.7 %all-to-all-start = ((f32[32,8,512]{2,1,0:T(8,128)}), f32[32,8,512]{2,1,0:T(8,128)S(1)}, u32[]{:S(2)}, u32[]{:S(2)}) async-start(f32[32,8,512]{2,1,0:T(8,128)} %fusion.16), calls=%async_computation | async-start | bytes 1048576 | tf_op jit(solution)/shard_map/all_to_all | solution.py:79
  36.7 25.1 %copy-start.8 = (f32[64,1024]{1,0:T(8,128)S(1)}, f32[64,1024]{1,0:T(8,128)}, u32[]{:S(2)}) copy-start(f32[64,1024]{1,0:T(8,128)} %param.13) | copy-start | bytes 786436
  52.2 38.1 %all-to-all-start.1 = ((f32[64,8,512]{2,1,0:T(8,128)}), f32[64,8,512]{2,1,0:T(8,128)}, u32[]{:S(2)}, u32[]{:S(2)}) async-start(f32[64,8,512]{2,1,0:T(8,128)} %broadcast_in_dim.7), calls=%async_computation.1 | async-start | bytes 2097152 | tf_op jit(solution)/shard_map/all_to_all | solution.py:87
  61.8 8.5 %collective-permute-start = (f32[64,1024]{1,0:T(8,128)S(1)}, f32[64,1024]{1,0:T(8,128)S(1)}, u32[]{:S(2)}, u32[]{:S(2)}) collective-permute-start(f32[64,1024]{1,0:T(8,128)S(1)} %copy-done.8), channel_id=1, source_target_pairs={{0,3},{1,0},{2,1},{3,2},{4,7},{5,4},{6,5},{7,6},{8,11},{9,8},{10,9... | collective-permute-start | bytes 786440 | tf_op jit(solution)/shard_map/ppermute | solution.py:95
  64.4 8.7 %collective-permute-start.1 = (f32[64,1024]{1,0:T(8,128)S(1)}, f32[64,1024]{1,0:T(8,128)S(1)}, u32[]{:S(2)}, u32[]{:S(2)}) collective-permute-start(f32[64,1024]{1,0:T(8,128)S(1)} %copy-done.8), channel_id=1, source_target_pairs={{0,2},{1,3},{2,0},{3,1},{4,6},{5,7},{6,4},{7,5},{8,10},{9,11},{10,... | collective-permute-start | bytes 786440 | tf_op jit(solution)/shard_map/ppermute | solution.py:95
  64.9 14.9 %collective-permute-start.2 = (f32[64,1024]{1,0:T(8,128)S(1)}, f32[64,1024]{1,0:T(8,128)S(1)}, u32[]{:S(2)}, u32[]{:S(2)}) collective-permute-start(f32[64,1024]{1,0:T(8,128)S(1)} %copy-done.8), channel_id=1, source_target_pairs={{0,1},{1,2},{2,3},{3,0},{4,5},{5,6},{6,7},{7,4},{8,9},{9,10},{10,1... | collective-permute-start | bytes 786440 | tf_op jit(solution)/shard_map/ppermute | solution.py:95
  100.6 2.0 %collective-permute-start.4 = (f32[32,8,512]{2,1,0:T(8,128)S(1)}, f32[32,8,512]{2,1,0:T(8,128)S(1)}, u32[]{:S(2)}, u32[]{:S(2)}) collective-permute-start(f32[32,8,512]{2,1,0:T(8,128)S(1)} %select_bitcast_fusion), channel_id=1, source_target_pairs={{0,4},{4,0},{1,5},{5,1},{2,6},{6,2},{3,7},{7,3},{8,12},{12,8},{9,1... | collective-permute-start | bytes 1572872 | tf_op jit(solution)/shard_map/ppermute | solution.py:78
  123.2 37.9 %all-to-all-start.3 = ((f32[64,8,512]{2,1,0:T(8,128)}), f32[64,8,512]{2,1,0:T(8,128)S(1)}, u32[]{:S(2)}, u32[]{:S(2)}) async-start(f32[64,8,512]{2,1,0:T(8,128)} %broadcast_in_dim.8), calls=%async_computation.3 | async-start | bytes 2097152 | tf_op jit(solution)/shard_map/all_to_all | solution.py:87
  162.9 5.4 %copy-start.4 = (f32[64,16,128]{2,0,1:T(8,128)S(1)}, f32[64,16,128]{2,0,1:T(8,128)}, u32[]{:S(2)}) copy-start(f32[64,16,128]{2,0,1:T(8,128)} %copy-done.3) | copy-start | bytes 1572868
  162.9 5.4 %copy-start.6 = (f32[64,16,128]{2,0,1:T(8,128)S(1)}, f32[64,16,128]{2,0,1:T(8,128)}, u32[]{:S(2)}) copy-start(f32[64,16,128]{2,0,1:T(8,128)} %copy-done.5) | copy-start | bytes 1572868
  168.3 2.6 %copy-start.2 = (f32[16,256,256]{2,1,0:T(8,128)S(1)}, f32[16,256,256]{2,1,0:T(8,128)}, u32[]{:S(2)}) copy-start(f32[16,256,256]{2,1,0:T(8,128)} %copy-done.1) | copy-start | bytes 12582916

commit v8 on v6

--- a/solution.py
+++ b/solution.py
@@ -13,23 +13,28 @@
 
 
 def scatter_rows(rows, updates, order):
-    count, columns = updates.shape
+    leaves, columns, touched = updates.shape
 
-    def kernel(rows_ref, upd_ref, out_ref):
+    def kernel(rows_ref, upd_ref, out_ref, rows_scratch):
         out_ref[...] = jnp.zeros_like(out_ref)
 
-        def body(group, carry):
-            base = group * GROUP
-            targets = [rows_ref[base + u] for u in range(GROUP)]
-            sums = [
-                out_ref[pl.ds(targets[u], 1), :] + upd_ref[pl.ds(base + u, 1), :]
-                for u in range(GROUP)
-            ]
-            for u in range(GROUP):
-                out_ref[pl.ds(targets[u], 1), :] = sums[u]
-            return carry
+        def leaf(index, carry):
+            rows_scratch[...] = upd_ref[index].T
 
-        lax.fori_loop(0, count // GROUP, body, 0)
+            def body(group, inner):
+                base = group * GROUP
+                targets = [rows_ref[index * touched + base + u] for u in range(GROUP)]
+                sums = [
+                    out_ref[pl.ds(targets[u], 1), :] + rows_scratch[pl.ds(base + u, 1), :]
+                    for u in range(GROUP)
+                ]
+                for u in range(GROUP):
+                    out_ref[pl.ds(targets[u], 1), :] = sums[u]
+                return inner
+
+            return lax.fori_loop(0, touched // GROUP, body, carry)
+
+        lax.fori_loop(0, leaves, leaf, 0)
 
     return pl.pallas_call(
         kernel,
@@ -37,8 +42,9 @@
         grid_spec=pltpu.PrefetchScalarGridSpec(
             num_scalar_prefetch=1,
             grid=(1,),
-            in_specs=[pl.BlockSpec((count, columns), lambda i, r: (0, 0))],
+            in_specs=[pl.BlockSpec((leaves, columns, touched), lambda i, r: (0, 0, 0))],
             out_specs=pl.BlockSpec((order, columns), lambda i, r: (0, 0)),
+            scratch_shapes=[pltpu.VMEM((touched, columns), jnp.float32)],
         ),
     )(rows, updates)
 
@@ -114,7 +120,7 @@
     masked = leaf_inverse * live_mask[:, :, None] * live_mask[:, None, :]
     leaf_forward_sweep = jnp.einsum("clt,lst->cls", leaf_rhs, masked, precision=largest_entry)
     update_terms = jnp.einsum(
-        "dwu,wqu->wqd", leaf_forward_sweep, leaf_offdiagonal_block, precision=largest_entry
+        "dwu,wqu->wdq", leaf_forward_sweep, leaf_offdiagonal_block, precision=largest_entry
     )
     root_full = gather_columns(root_inverse)
     root_order = root_full.shape[1]
@@ -122,9 +128,7 @@
     blocks = root_order // width
     flat_rows = update_rows.reshape(-1)
     assert touched % GROUP == 0
-    accumulated_sum = scatter_rows(
-        flat_rows, update_terms.reshape(leaf_count * touched, columns), root_order
-    )
+    accumulated_sum = scatter_rows(flat_rows, update_terms, root_order)
     shares = owner_sum(accumulated_sum.reshape(blocks, width, columns))
     reduced = root_rhs.T - shares
     forward_root = jnp.einsum(

time: 173 us -> 174 us (level)
  no operation moved by 1% of the time
where the time goes in v8:
time: 174 us
  waiting for transfers between devices  62.8 us (36%)
  starting transfers between devices  35.7 us (21%)
  local copies, waits for them, and re-layouts  21.3 us (12%)
  blocking collectives  19.4 us (11%)
  matrix products  17.4 us (10%)
  Pallas kernels  14 us (8%)
  other arithmetic  2.22 us (1%)
    all_to_all x2, waiting for transfers between devices, share_all(): gathered = lax.all_to_all(copies, LEAF_AXES, 0, 0, tiled=False)  33.1 us
    all_to_all x1, blocking collectives, owner_sum(): spread = lax.all_to_all(paired, ('y', 'z'), 0, 0, tiled=False)  19.4 us
    all_to_all x2, starting transfers between devices, share_all(): gathered = lax.all_to_all(copies, LEAF_AXES, 0, 0, tiled=False)  19 us
    all_to_all x1, waiting for transfers between devices, owner_sum(): spread = lax.all_to_all(paired, ('y', 'z'), 0, 0, tiled=False)  14.1 us
    ppermute x3, waiting for transfers between devices, gather_columns(): lax.ppermute(part, 'rhs', [(i, (i + step) % count) for i in range(count)])  12.2 us
    unnamed x23, local copies, waits for them, and re-layouts  9.7 us
    all_to_all x1, starting transfers between devices, owner_sum(): spread = lax.all_to_all(paired, ('y', 'z'), 0, 0, tiled=False)  9.5 us
    pallas_call x1, Pallas kernels, scatter_rows(): pl.pallas_call(kernel, out_shape=jax.ShapeDtypeStruct((order, columns), j...  8.62 us
  transfers between devices with their start and end apart: 8, of which 8 were waited for; matrix products, arithmetic and copies ran while one was open for 5% of the time, Pallas kernels for 0%

profile of v8, /device:TPU:1, one launch (start us, length us, event | category | flops | bytes accessed | tf_op | source)
XLA Modules:
  0.0 173.5 jit_solution(10637248864125916330)
XLA Ops:
  1.5 5.3 %fusion.6 = f32[64,16,256]{2,0,1:T(8,128)S(1)} fusion(f32[16,256,256]{2,1,0:T(8,128)} %param.9, f32[16,256]{1,0:T(8,128)S(1)} %fusion.12, f32[64,16,256]{2,1,0:T(8,128)} %param.7), kind=kOutput, calls=%fused_computation.7 | convolution fusion | flops 404750336 | bytes 6307840 | tf_op jit(solution)/shard_map/clt,lst->cls/dot_general | solution.py:121
  6.9 1.0 copy-done.2
  7.9 2.0 %fusion.13.upd_ref = f32[16,64,128]{2,1,0:T(8,128)} fusion(f32[64,16,256]{2,0,1:T(8,128)S(1)} %fusion.6, f32[16,128,256]{2,1,0:T(8,128)S(1)} %copy-done), kind=kOutput, calls=%fused_computation.32 | convolution fusion | flops 201326592 | bytes 3670016 | tf_op jit(solution)/shard_map/dwu,wqu->wdq/dot_general | solution.py:122
  9.9 8.6 %shard_map.86 = f32[4096,64]{1,0:T(8,128)} custom-call(s32[2048]{0:T(1024)} %bitcast.76, f32[16,64,128]{2,1,0:T(8,128)} %fusion.13.upd_ref), custom_call_target="tpu_custom_call" | custom-call | tf_op jit(solution)/shard_map/pallas_call | solution.py:39
  18.5 1.9 %reshape_reshape.7 = f32[32,2,8,512]{3,2,1,0:T(8,128)S(1)} reshape(f32[4096,64]{1,0:T(8,128)} %shard_map.86) | data formatting | bytes 2097152 | tf_op jit(solution)/shard_map/reshape;reshape | solution.py:81
  20.5 3.3 %collective-permute-start.3 = (f32[32,8,512]{2,1,0:T(8,128)S(1)}, f32[32,8,512]{2,1,0:T(8,128)S(1)}, u32[]{:S(2)}, u32[]{:S(2)}) collective-permute-start(f32[32,8,512]{2,1,0:T(8,128)S(1)} %select_bitcast_fusion.1), channel_id=1, source_target_pairs={{0,4},{4,0},{1,5},{5,1},{2,6},{6,2},{3,7},{7,3},{8,12},{12,8},{9,1... | collective-permute-start | bytes 1572872 | tf_op jit(solution)/shard_map/ppermute | solution.py:84
  23.8 1.5 collective-permute-done.3
  25.4 0.9 fusion.11
  26.3 9.5 %all-to-all-start = ((f32[32,8,512]{2,1,0:T(8,128)}), f32[32,8,512]{2,1,0:T(8,128)S(1)}, u32[]{:S(2)}, u32[]{:S(2)}) async-start(f32[32,8,512]{2,1,0:T(8,128)} %fusion.11), calls=%async_computation | async-start | bytes 1048576 | tf_op jit(solution)/shard_map/all_to_all | solution.py:85
  35.9 14.1 %all-to-all-done = f32[32,8,512]{2,1,0:T(8,128)S(1)} async-done(((f32[32,8,512]{2,1,0:T(8,128)}), f32[32,8,512]{2,1,0:T(8,128)S(1)}, u32[]{:S(2)}, u32[]{:S(2)}) %all-to-all-start) | async-done | bytes 524320 | tf_op jit(solution)/shard_map/all_to_all | solution.py:85
  50.2 1.1 broadcast_in_dim.7
  51.3 9.6 %all-to-all-start.1 = ((f32[64,8,512]{2,1,0:T(8,128)}), f32[64,8,512]{2,1,0:T(8,128)}, u32[]{:S(2)}, u32[]{:S(2)}) async-start(f32[64,8,512]{2,1,0:T(8,128)} %broadcast_in_dim.7), calls=%async_computation.1 | async-start | bytes 2097152 | tf_op jit(solution)/shard_map/all_to_all | solution.py:93
  60.9 2.6 %collective-permute-start = (f32[64,1024]{1,0:T(8,128)S(1)}, f32[64,1024]{1,0:T(8,128)S(1)}, u32[]{:S(2)}, u32[]{:S(2)}) collective-permute-start(f32[64,1024]{1,0:T(8,128)S(1)} %copy-done.4), channel_id=1, source_target_pairs={{0,3},{1,0},{2,1},{3,2},{4,7},{5,4},{6,5},{7,6},{8,11},{9,8},{10,9... | collective-permute-start | bytes 786440 | tf_op jit(solution)/shard_map/ppermute | solution.py:101
  65.4 4.1 %collective-permute-done = f32[64,1024]{1,0:T(8,128)S(1)} collective-permute-done((f32[64,1024]{1,0:T(8,128)S(1)}, f32[64,1024]{1,0:T(8,128)S(1)}, u32[]{:S(2)}, u32[]{:S(2)}) %collective-permute-start) | collective-permute-done | bytes 262176 | tf_op jit(solution)/shard_map/ppermute | solution.py:101
  70.1 2.1 %collective-permute-done.1 = f32[64,1024]{1,0:T(8,128)S(1)} collective-permute-done((f32[64,1024]{1,0:T(8,128)S(1)}, f32[64,1024]{1,0:T(8,128)S(1)}, u32[]{:S(2)}, u32[]{:S(2)}) %collective-permute-start.1) | collective-permute-done | bytes 262176 | tf_op jit(solution)/shard_map/ppermute | solution.py:101
  72.9 6.0 %collective-permute-done.2 = f32[64,1024]{1,0:T(8,128)S(1)} collective-permute-done((f32[64,1024]{1,0:T(8,128)S(1)}, f32[64,1024]{1,0:T(8,128)S(1)}, u32[]{:S(2)}, u32[]{:S(2)}) %collective-permute-start.2) | collective-permute-done | bytes 262176 | tf_op jit(solution)/shard_map/ppermute | solution.py:101
  82.6 1.3 dynamic-slice_bitcast_fusion
  84.0 5.4 %all-to-all-done.1 = f32[64,8,512]{2,1,0:T(8,128)} async-done(((f32[64,8,512]{2,1,0:T(8,128)}), f32[64,8,512]{2,1,0:T(8,128)}, u32[]{:S(2)}, u32[]{:S(2)}) %all-to-all-start.1) | async-done | bytes 1048608 | tf_op jit(solution)/shard_map/all_to_all | solution.py:93
  89.4 2.7 %reshape.73 = f32[4096,64]{1,0:T(8,128)} reshape(f32[64,8,512]{2,1,0:T(8,128)} %all-to-all-done.1) | data formatting | bytes 2097152 | tf_op jit(solution)/shard_map/reshape | solution.py:94
  92.1 2.4 %fusion.14 = f32[64,64]{1,0:T(8,128)S(1)} fusion(f32[64,4096]{1,0:T(8,128)S(1)} %bitcast.72, f32[4096,64]{1,0:T(8,128)} %reshape.73), kind=kOutput, calls=%fused_computation.33 | convolution fusion | flops 100663296 | bytes 2113536 | tf_op jit(solution)/shard_map/jc,ij->ic/dot_general | solution.py:134
  94.5 3.1 %fusion.15 = f32[4096,64]{1,0:T(8,128)} fusion(f32[64,4096]{1,0:T(8,128)S(1)} %bitcast.73, f32[64,64]{1,0:T(8,128)S(1)} %fusion.14), kind=kOutput, calls=%fused_computation.34 | convolution fusion | flops 100663296 | bytes 2113536 | tf_op jit(solution)/shard_map/ic,ij->jc/dot_general | solution.py:140
  97.6 1.9 %reshape_reshape.8 = f32[32,2,8,512]{3,2,1,0:T(8,128)S(1)} reshape(f32[4096,64]{1,0:T(8,128)} %fusion.15) | data formatting | bytes 2097152 | tf_op jit(solution)/shard_map/reshape;reshape | solution.py:81
  99.8 1.8 %collective-permute-done.4 = f32[32,8,512]{2,1,0:T(8,128)S(1)} collective-permute-done((f32[32,8,512]{2,1,0:T(8,128)S(1)}, f32[32,8,512]{2,1,0:T(8,128)S(1)}, u32[]{:S(2)}, u32[]{:S(2)}) %collective-permute-start.4) | collective-permute-done | bytes 524320 | tf_op jit(solution)/shard_map/ppermute | solution.py:84
  101.8 19.4 %all_to_all.20 = f32[32,8,512]{2,1,0:T(8,128)S(1)} all-to-all(f32[32,8,512]{2,1,0:T(8,128)S(1)} %bitcast_add_fusion), channel_id=1, replica_groups=mesh['y'=4,'z'=8,'core'=2,'rhs'=4] {'y','z'}, dimensions={0} | all-to-all | bytes 1048576 | tf_op jit(solution)/shard_map/all_to_all | solution.py:85
  121.2 1.1 broadcast_in_dim.8
  122.3 9.4 %all-to-all-start.3 = ((f32[64,8,512]{2,1,0:T(8,128)}), f32[64,8,512]{2,1,0:T(8,128)S(1)}, u32[]{:S(2)}, u32[]{:S(2)}) async-start(f32[64,8,512]{2,1,0:T(8,128)} %broadcast_in_dim.8), calls=%async_computation.3 | async-start | bytes 2097152 | tf_op jit(solution)/shard_map/all_to_all | solution.py:93
  132.5 27.7 %all-to-all-done.3 = f32[64,8,512]{2,1,0:T(8,128)S(1)} async-done(((f32[64,8,512]{2,1,0:T(8,128)}), f32[64,8,512]{2,1,0:T(8,128)S(1)}, u32[]{:S(2)}, u32[]{:S(2)}) %all-to-all-start.3) | async-done | bytes 1048608 | tf_op jit(solution)/shard_map/all_to_all | solution.py:93
  160.3 1.7 %reshape.74.table_ref = f32[4096,64]{1,0:T(8,128)} reshape(f32[64,8,512]{2,1,0:T(8,128)S(1)} %all-to-all-done.3) | data formatting | bytes 2097152 | tf_op jit(solution)/shard_map/reshape | solution.py:94
  162.0 5.4 %shard_map.87 = f32[2048,64]{1,0:T(8,128)} custom-call(s32[2048]{0:T(1024)} %bitcast.77, f32[4096,64]{1,0:T(8,128)} %reshape.74.table_ref), custom_call_target="tpu_custom_call" | custom-call | tf_op jit(solution)/shard_map/pallas_call | solution.py:66
  167.4 2.6 %fusion.8 = f32[64,16,256]{2,0,1:T(8,128)S(1)} fusion(f32[64,16,256]{2,0,1:T(8,128)S(1)} %copy-done.3, f32[16,128,64]{2,1,0:T(8,128)} %bitcast.74, f32[16,128,256]{2,1,0:T(8,128)S(1)} %copy-done), kind=kOutput, calls=%fused_computation.10 | convolution fusion | flops 201588736 | bytes 4718592 | tf_op jit(solution)/shard_map/nvr,nvb->rnb/dot_general | solution.py:144
  170.0 1.9 %fusion.7 = f32[64,16,256]{2,0,1:T(8,128)S(1)} fusion(f32[64,16,256]{2,0,1:T(8,128)S(1)} %fusion.8, f32[16,256,256]{2,1,0:T(8,128)S(1)} %copy-done.1, f32[16,256]{1,0:T(8,128)S(1)} %fusion.12), kind=kOutput, calls=%fused_computation.8 | convolution fusion | flops 404750336 | bytes 6307840 | tf_op jit(solution)/shard_map/cls,lst->clt/dot_general | solution.py:147
  172.0 1.6 copy.25
  (35 shorter events, 9.4 us)
Async XLA Ops:
  0.6 7.2 %copy-start = (f32[16,128,256]{2,1,0:T(8,128)S(1)}, f32[16,128,256]{2,1,0:T(8,128)}, u32[]{:S(2)}) copy-start(f32[16,128,256]{2,1,0:T(8,128)} %param.10) | copy-start | bytes 6291460
  6.9 1.0 copy-start.2
  20.4 15.4 %copy-start.5 = (f32[64,64]{1,0:T(8,128)S(1)}, f32[64,64]{1,0:T(8,128)}, u32[]{:S(2)}) copy-start(f32[64,64]{1,0:T(8,128)} %param.8) | copy-start | bytes 49156
  20.5 4.8 %collective-permute-start.3 = (f32[32,8,512]{2,1,0:T(8,128)S(1)}, f32[32,8,512]{2,1,0:T(8,128)S(1)}, u32[]{:S(2)}, u32[]{:S(2)}) collective-permute-start(f32[32,8,512]{2,1,0:T(8,128)S(1)} %select_bitcast_fusion.1), channel_id=1, source_target_pairs={{0,4},{4,0},{1,5},{5,1},{2,6},{6,2},{3,7},{7,3},{8,12},{12,8},{9,1... | collective-permute-start | bytes 1572872 | tf_op jit(solution)/shard_map/ppermute | solution.py:84
  26.3 23.7 %all-to-all-start = ((f32[32,8,512]{2,1,0:T(8,128)}), f32[32,8,512]{2,1,0:T(8,128)S(1)}, u32[]{:S(2)}, u32[]{:S(2)}) async-start(f32[32,8,512]{2,1,0:T(8,128)} %fusion.11), calls=%async_computation | async-start | bytes 1048576 | tf_op jit(solution)/shard_map/all_to_all | solution.py:85
  35.8 25.1 %copy-start.4 = (f32[64,1024]{1,0:T(8,128)S(1)}, f32[64,1024]{1,0:T(8,128)}, u32[]{:S(2)}) copy-start(f32[64,1024]{1,0:T(8,128)} %param.13) | copy-start | bytes 786436
  51.3 38.1 %all-to-all-start.1 = ((f32[64,8,512]{2,1,0:T(8,128)}), f32[64,8,512]{2,1,0:T(8,128)}, u32[]{:S(2)}, u32[]{:S(2)}) async-start(f32[64,8,512]{2,1,0:T(8,128)} %broadcast_in_dim.7), calls=%async_computation.1 | async-start | bytes 2097152 | tf_op jit(solution)/shard_map/all_to_all | solution.py:93
  60.9 8.5 %collective-permute-start = (f32[64,1024]{1,0:T(8,128)S(1)}, f32[64,1024]{1,0:T(8,128)S(1)}, u32[]{:S(2)}, u32[]{:S(2)}) collective-permute-start(f32[64,1024]{1,0:T(8,128)S(1)} %copy-done.4), channel_id=1, source_target_pairs={{0,3},{1,0},{2,1},{3,2},{4,7},{5,4},{6,5},{7,6},{8,11},{9,8},{10,9... | collective-permute-start | bytes 786440 | tf_op jit(solution)/shard_map/ppermute | solution.py:101
  63.5 8.7 %collective-permute-start.1 = (f32[64,1024]{1,0:T(8,128)S(1)}, f32[64,1024]{1,0:T(8,128)S(1)}, u32[]{:S(2)}, u32[]{:S(2)}) collective-permute-start(f32[64,1024]{1,0:T(8,128)S(1)} %copy-done.4), channel_id=1, source_target_pairs={{0,2},{1,3},{2,0},{3,1},{4,6},{5,7},{6,4},{7,5},{8,10},{9,11},{10,... | collective-permute-start | bytes 786440 | tf_op jit(solution)/shard_map/ppermute | solution.py:101
  64.0 14.9 %collective-permute-start.2 = (f32[64,1024]{1,0:T(8,128)S(1)}, f32[64,1024]{1,0:T(8,128)S(1)}, u32[]{:S(2)}, u32[]{:S(2)}) collective-permute-start(f32[64,1024]{1,0:T(8,128)S(1)} %copy-done.4), channel_id=1, source_target_pairs={{0,1},{1,2},{2,3},{3,0},{4,5},{5,6},{6,7},{7,4},{8,9},{9,10},{10,1... | collective-permute-start | bytes 786440 | tf_op jit(solution)/shard_map/ppermute | solution.py:101
  99.7 2.0 %collective-permute-start.4 = (f32[32,8,512]{2,1,0:T(8,128)S(1)}, f32[32,8,512]{2,1,0:T(8,128)S(1)}, u32[]{:S(2)}, u32[]{:S(2)}) collective-permute-start(f32[32,8,512]{2,1,0:T(8,128)S(1)} %select_bitcast_fusion), channel_id=1, source_target_pairs={{0,4},{4,0},{1,5},{5,1},{2,6},{6,2},{3,7},{7,3},{8,12},{12,8},{9,1... | collective-permute-start | bytes 1572872 | tf_op jit(solution)/shard_map/ppermute | solution.py:84
  122.3 37.9 %all-to-all-start.3 = ((f32[64,8,512]{2,1,0:T(8,128)}), f32[64,8,512]{2,1,0:T(8,128)S(1)}, u32[]{:S(2)}, u32[]{:S(2)}) async-start(f32[64,8,512]{2,1,0:T(8,128)} %broadcast_in_dim.8), calls=%async_computation.3 | async-start | bytes 2097152 | tf_op jit(solution)/shard_map/all_to_all | solution.py:93
  162.0 5.4 %copy-start.3 = (f32[64,16,256]{2,0,1:T(8,128)S(1)}, f32[64,16,256]{2,0,1:T(8,128)}, u32[]{:S(2)}) copy-start(f32[64,16,256]{2,0,1:T(8,128)} %copy-done.2) | copy-start | bytes 3145732
  167.4 2.6 %copy-start.1 = (f32[16,256,256]{2,1,0:T(8,128)S(1)}, f32[16,256,256]{2,1,0:T(8,128)}, u32[]{:S(2)}) copy-start(f32[16,256,256]{2,1,0:T(8,128)} %param.9) | copy-start | bytes 12582916
